TPU v7x, 128 devices: a whole 4x4x4 slice. The times are simulated.
128 devices in a mesh: body: 4 (over x), dom: 32 (over y, z, core).
Axes of the slice: x: 4, y: 4, z: 4, core: 2. Of those that a mesh axis runs over, the one named last changes fastest.
Arguments:
- master_basis: bfloat16 [65536, 16, 256], P(('body', 'dom')), may hold values from -1.5 to 1.5
- master_weights: bfloat16 [65536, 4, 16], P(('body', 'dom')), may hold values from 0.099609375 to 1
- master_dest: int32 [65536, 1], P(('body', 'dom')), may hold values from 0 to 31; in each aligned block of 512 rows (0 to 511, 512 to 1023, ...) at most 32 rows name the same one
- master_slaves: int32 [65536, 4], P(('body', 'dom')), may hold values from 0 to 511
- slave_basis: bfloat16 [65536, 16, 256], P(('body', 'dom')), may hold values from -1.5 to 1.5
- slave_gain: float32 [65536], P(('body', 'dom')), may hold values from 0.1 to 1
- tile_owner: int32 [4096, 1], P(('body', 'dom')), may hold values from 0 to 31; in each aligned block of 32 rows (0 to 31, 32 to 63, ...) at most 2 rows name the same one
- tile_row: int32 [4096], P(('body', 'dom')), may hold values from 0 to 15
Outputs:
- coupling: float32 [2048, 256, 256], P(('body', 'dom'))
Inputs may be any that keep to these rules, and one draw needn't show every extreme that they name: `master_dest`: among the master segments of one device at most 32 name the same dom index, and that many is reached. `tile_owner`: among the tiles of one device at most 2 name the same owner, and that many is reached.
All inputs are finite; a program needn't handle non-finite values.
Results may differ from a plain program's by a relative error of at most 0.0027.
Values may be sent and summed in bfloat16 or wider, within the bound.
No kernel may reach another device: no remote copies, remote signals or barrier semaphores. Data moves between devices by JAX's collectives and lax.ppermute only.
A program may use at most 256 MiB of HBM per device.

v0:
```python
import functools

import jax
import jax.numpy as jnp
from jax import lax
from jax.experimental import pallas as pl
from jax.experimental.pallas import tpu as pltpu
from jax.sharding import PartitionSpec as P

NP = 256
Q = 16
PAIRS = 4
BR = 16
SPLIT = 2


def shifted(block, axis, distance):
    devices = range(lax.axis_size(axis))
    route = [((i - distance) % len(devices), i) for i in devices]
    return lax.ppermute(block, axis, route)


def slot_of(target, groups, capacity):
    onehot = (target[:, None] == jnp.arange(groups, dtype=jnp.int32)[None, :]).astype(jnp.int32)
    before = jnp.cumsum(onehot, axis=0) - onehot
    position = jnp.sum(before * onehot, axis=1)
    return target * capacity + position


def placer_of(slot, slots):
    return slot[None, :] == jnp.arange(slots, dtype=jnp.int32)[:, None]


def flux_kernel(hi_ref, lo_ref, rows_ref, own_ref, scale_ref, out_ref):
    rows = rows_ref[...]
    far = jnp.dot(hi_ref[0], rows, preferred_element_type=jnp.float32)
    far = far + jnp.dot(lo_ref[0], rows, preferred_element_type=jnp.float32)
    out_ref[0] = (scale_ref[0] * own_ref[0].astype(jnp.float32) - far).astype(jnp.bfloat16)


def flux_chunk(table_hi, table_lo, rows, own, scale, chunk):
    q_count, slave_count, slots = table_hi.shape
    width = rows.shape[1] // q_count
    return pl.pallas_call(
        flux_kernel,
        grid=(q_count,),
        in_specs=[
            pl.BlockSpec((1, slave_count, slots), lambda q: (q, 0, 0)),
            pl.BlockSpec((1, slave_count, slots), lambda q: (q, 0, 0)),
            pl.BlockSpec((slots, width), lambda q: (0, q)),
            pl.BlockSpec((1, slave_count, width), lambda q: (q, 0, chunk)),
            pl.BlockSpec((1, slave_count, 1), lambda q: (q, 0, 0)),
        ],
        out_specs=pl.BlockSpec((1, slave_count, width), lambda q: (q, 0, 0)),
        out_shape=jax.ShapeDtypeStruct((q_count, slave_count, width), jnp.bfloat16),
    )(table_hi, table_lo, rows, own, scale)


def tile_kernel(tile_count, source_ref, left_ref, flux_ref, out_ref):
    x = pl.program_id(0)
    real = source_ref[x] < tile_count

    @pl.when(real)
    def _():
        q_count, per_tile, width = flux_ref.shape
        right = flux_ref[...].reshape(q_count * per_tile, width)
        out_ref[0] = jnp.dot(left_ref[0], right, preferred_element_type=jnp.float32).astype(jnp.bfloat16)

    @pl.when(jnp.logical_not(real))
    def _():
        out_ref[...] = jnp.zeros(out_ref.shape, out_ref.dtype)


def packed_tiles_of(source, left, flux, per_tile):
    tile_slots = source.shape[0]
    tile_count, rows, depth = left.shape
    q_count, slave_count, width = flux.shape
    last = tile_count - 1
    grid_spec = pltpu.PrefetchScalarGridSpec(
        num_scalar_prefetch=1,
        grid=(tile_slots,),
        in_specs=[
            pl.BlockSpec((1, rows, depth), lambda x, src: (jnp.minimum(src[x], last), 0, 0)),
            pl.BlockSpec((q_count, per_tile, width), lambda x, src: (0, jnp.minimum(src[x], last), 0)),
        ],
        out_specs=pl.BlockSpec((1, rows, width), lambda x, src: (x, 0, 0)),
    )
    return pl.pallas_call(
        functools.partial(tile_kernel, tile_count),
        grid_spec=grid_spec,
        out_shape=jax.ShapeDtypeStruct((tile_slots, rows, width), jnp.bfloat16),
    )(source, left, flux)


def on_device(
    master_basis,
    master_weights,
    master_dest,
    master_slaves,
    slave_basis,
    slave_gain,
    tile_owner,
    tile_row,
):
    f32, bf16, i32 = jnp.float32, jnp.bfloat16, jnp.int32
    dom_count = lax.axis_size("dom")
    seg_count = master_basis.shape[0]
    capacity = 2 * seg_count // dom_count
    slots = dom_count * capacity
    slave_count = slave_basis.shape[0]
    tile_count = tile_row.shape[0]
    per_tile = slave_count // tile_count
    tile_capacity = max(2, 2 * tile_count // dom_count)
    tile_slots = dom_count * tile_capacity
    width = NP // SPLIT
    wcols = PAIRS * Q

    meta = jnp.concatenate(
        [
            master_weights.reshape(seg_count, wcols).astype(f32),
            master_dest.astype(f32),
            master_slaves.astype(f32) + 1.0,
        ],
        axis=1,
    )
    moved_meta = shifted(meta, "body", 1)
    moved_chunks = []
    for k in range(SPLIT):
        piece = master_basis[:, :, k * width:(k + 1) * width]
        if moved_chunks:
            piece, _ = lax.optimization_barrier((piece, moved_chunks[-1]))
        moved_chunks.append(shifted(piece, "body", 1))

    moved_dest = moved_meta[:, wcols].astype(i32)
    slot = slot_of(moved_dest, dom_count, capacity)
    placer = placer_of(slot, slots)
    records = jnp.concatenate([moved_meta[:, :wcols], moved_meta[:, wcols + 1:]], axis=1)
    packed_meta = jnp.dot(placer.astype(f32), records, precision=lax.Precision.HIGHEST)
    rec_cols = records.shape[1]

    tile_slot = slot_of(tile_owner[:, 0], dom_count, tile_capacity)
    tile_placer = placer_of(tile_slot, tile_slots)
    packed_rows = jnp.dot(tile_placer.astype(i32), tile_row + 1).astype(f32)

    send_meta = jnp.concatenate(
        [
            packed_meta.reshape(dom_count, capacity * rec_cols),
            packed_rows.reshape(dom_count, tile_capacity),
        ],
        axis=1,
    )
    got_meta = lax.all_to_all(send_meta, "dom", 0, 0, tiled=True)

    got_chunks = []
    for k in range(SPLIT):
        packed = jnp.dot(
            placer.astype(bf16),
            moved_chunks[k].reshape(seg_count, Q * width),
            preferred_element_type=f32,
        ).astype(bf16)
        got_chunks.append(
            lax.all_to_all(packed.reshape(dom_count, capacity, Q * width), "dom", 0, 0, tiled=True)
        )

    got_records = got_meta[:, : capacity * rec_cols].reshape(slots, rec_cols)
    got_weights = got_records[:, :wcols].reshape(slots, PAIRS, Q)
    got_owners = got_records[:, wcols:].astype(i32) - 1
    slave_ids = jnp.arange(slave_count, dtype=i32)
    table = None
    for p in range(PAIRS):
        term = jnp.where(
            got_owners[None, None, :, p] == slave_ids[None, :, None],
            jnp.transpose(got_weights[:, p, :])[:, None, :],
            0.0,
        )
        table = term if table is None else table + term
    table_hi = table.astype(bf16)
    table_lo = (table - table_hi.astype(f32)).astype(bf16)
    weight_sum = jnp.sum(table, axis=2)
    table_hi, table_lo, weight_sum = lax.optimization_barrier((table_hi, table_lo, weight_sum))
    scale = (jnp.transpose(slave_gain[:, None]) + weight_sum)[:, :, None]

    got_rows = got_meta[:, capacity * rec_cols:].reshape(tile_slots).astype(i32) - 1
    selector = (got_rows[None, :] == jnp.arange(BR, dtype=i32)[:, None]).astype(bf16)
    tile_source = jnp.dot(tile_placer.astype(i32), jnp.arange(1, tile_count + 1, dtype=i32)) - 1
    tile_source = jnp.where(tile_source < 0, tile_count, tile_source)
    own = jnp.transpose(slave_basis, (1, 0, 2))
    left = jnp.transpose(
        slave_basis.reshape(tile_count, per_tile, Q, NP), (0, 3, 2, 1)
    ).reshape(tile_count, NP, Q * per_tile)

    parts = []
    for k in range(SPLIT):
        rows = got_chunks[k].reshape(slots, Q * width)
        flux = flux_chunk(table_hi, table_lo, rows, own, scale, k)
        packed_tiles = packed_tiles_of(tile_source, left, flux, per_tile)
        got_tiles = lax.all_to_all(
            packed_tiles.reshape(dom_count, tile_capacity * NP, width), "dom", 0, 0, tiled=True
        )
        part = jnp.einsum(
            "bx,xnm->bnm",
            selector,
            got_tiles.reshape(tile_slots, NP, width),
            preferred_element_type=f32,
        )
        parts.append(part)
    return jnp.concatenate(parts, axis=2)


def solution(mesh):
    return jax.shard_map(
        on_device,
        mesh=mesh,
        in_specs=(
            P(("body", "dom"), None, None),
            P(("body", "dom"), None, None),
            P(("body", "dom"), None),
            P(("body", "dom"), None),
            P(("body", "dom"), None, None),
            P(("body", "dom")),
            P(("body", "dom"), None),
            P(("body", "dom")),
        ),
        out_specs=P(("body", "dom"), None, None),
        check_vma=False,
    )
```

profile of v0, /device:TPU:32, one launch (start us, length us, event | category | flops | bytes accessed | tf_op | source)
XLA Modules:
  0.0 360.1 jit_solution(10452077000827073786)
XLA Ops:
  2.3 1.6 collective-permute-start
  3.8 4.3 %fusion.39 = (bf16[512,16,128]{2,1,0:T(8,128)(2,1)}, bf16[512,16,128]{2,1,0:T(8,128)(2,1)S(1)}) fusion(bf16[512,16,256]{2,1,0:T(8,128)(2,1)} %param.8), kind=kLoop, calls=%fused_computation.81 | loop fusion | bytes 8388608 | tf_op jit(solution)/shard_map/slice | solution.py:129
  14.2 8.2 %all-to-all-start = ((f32[32,1,2178]{2,1,0:T(1,128)}), f32[32,1,2178]{2,1,0:T(1,128)S(1)}, u32[]{:S(2)}, u32[]{:S(2)}) async-start(f32[32,1,2178]{2,1,0:T(1,128)} %copy.41), calls=%async_computation | async-start | bytes 589824 | tf_op jit(solution)/shard_map/all_to_all | solution.py:152
  22.4 34.3 %collective-permute-done.1 = bf16[512,16,128]{2,1,0:T(8,128)(2,1)} collective-permute-done((bf16[512,16,128]{2,1,0:T(8,128)(2,1)}, bf16[512,16,128]{2,1,0:T(8,128)(2,1)}, u32[]{:S(2)}, u32[]{:S(2)}) %collective-permute-start.1) | collective-permute-done | bytes 2097184 | tf_op jit(solution)/shard_map/ppermute | solution.py:20
  56.7 5.9 %convolution_convert_fusion.1 = bf16[1024,2048]{1,0:T(8,128)(2,1)} fusion(bf16[64,8,16,128]{3,2,1,0:T(8,128)(2,1)} %bitcast.43, s32[512]{0:T(512)S(1)} %add.53), kind=kOutput, calls=%fused_computation.11 | convolution fusion | flops 2150105088 | bytes 6293504 | tf_op jit(solution)/shard_map/dot_general | solution.py:156
  62.6 8.3 %all-to-all-start.1 = ((bf16[32,32,2048]{2,1,0:T(8,128)(2,1)}), bf16[32,32,2048]{2,1,0:T(8,128)(2,1)}, u32[]{:S(2)}, u32[]{:S(2)}) async-start(bf16[32,32,2048]{2,1,0:T(8,128)(2,1)} %bitcast.103), calls=%async_computation.1 | async-start | bytes 8388608 | tf_op jit(solution)/shard_map/all_to_all | solution.py:162
  71.4 5.9 %copy.72 = bf16[512,16,256]{2,0,1:T(8,128)(2,1)} copy(bf16[512,16,256]{2,1,0:T(8,128)(2,1)} %param.12) | data formatting | bytes 8388608 | tf_op args[4]
  77.3 3.9 %copy.42 = bf16[32,256,16,16]{1,3,2,0:T(8,128)(2,1)} copy(bf16[32,256,16,16]{1,2,3,0:T(8,128)(2,1)S(1)} %bitcast.97) | data formatting | bytes 8388608 | tf_op jit(solution)/shard_map/transpose | solution.py:188
  81.2 6.5 %copy.46.left_ref = bf16[32,256,256]{2,1,0:T(8,128)(2,1)} copy(bf16[32,256,256]{1,2,0:T(8,128)(2,1)} %bitcast.100) | data formatting | bytes 8388608 | tf_op jit(solution)/shard_map/reshape | solution.py:190
  90.3 29.8 %collective-permute-done.2 = bf16[512,16,128]{2,1,0:T(8,128)(2,1)} collective-permute-done((bf16[512,16,128]{2,1,0:T(8,128)(2,1)S(1)}, bf16[512,16,128]{2,1,0:T(8,128)(2,1)}, u32[]{:S(2)}, u32[]{:S(2)}) %collective-permute-start.2) | collective-permute-done | bytes 2097184 | tf_op jit(solution)/shard_map/ppermute | solution.py:20
  120.1 6.0 %convolution_convert_fusion = bf16[1024,2048]{1,0:T(8,128)(2,1)} fusion(bf16[64,8,16,128]{3,2,1,0:T(8,128)(2,1)} %bitcast.45, s32[512]{0:T(512)S(1)} %add.53), kind=kOutput, calls=%fused_computation.10 | convolution fusion | flops 2150105088 | bytes 6293504 | tf_op jit(solution)/shard_map/dot_general | solution.py:156
  126.0 7.6 %all-to-all-start.3 = ((bf16[32,32,2048]{2,1,0:T(8,128)(2,1)}), bf16[32,32,2048]{2,1,0:T(8,128)(2,1)}, u32[]{:S(2)}, u32[]{:S(2)}) async-start(bf16[32,32,2048]{2,1,0:T(8,128)(2,1)} %bitcast.102), calls=%async_computation.3 | async-start | bytes 8388608 | tf_op jit(solution)/shard_map/all_to_all | solution.py:162
  136.0 24.2 %fusion = (f32[16,512]{1,0:T(8,128)S(1)}, bf16[16,512,1024]{2,1,0:T(8,128)(2,1)}, bf16[16,512,1024]{2,1,0:T(8,128)(2,1)}) fusion(f32[16,1024]{1,0:T(8,128)S(1)} %get-tuple-element.23, f32[16,1024]{1,0:T(8,128)S(1)} %get-tuple-element.24, f32[16,1024]{1,0:T(8,128)S(1)} %get-tuple-element.25, f32[16,1024]{1,0:T(8,128)S(1)} %get-tuple-element.22, ...), kind=kLoop, calls=%fused_computation.2 | loop fusion | flops 100655104 | bytes 35946496 | tf_op jit(solution)/shard_map/reduce_sum | solution.py:179
  160.2 2.6 copy.45.scale_ref
  162.8 22.5 %shard_map.82.flux_ref = bf16[16,512,128]{2,1,0:T(8,128)(2,1)} custom-call(bf16[16,512,1024]{2,1,0:T(8,128)(2,1)} %get-tuple-element.9.hi_ref, bf16[16,512,1024]{2,1,0:T(8,128)(2,1)} %get-tuple-element.10.lo_ref, bf16[1024,2048]{1,0:T(8,128)(2,1)} %bitcast.25.rows_ref, bf16[16,512,256]{2,1,0:T(8,128)(2,1)} %bitcast.95, f32[16,512,1]{2,1,0:T(8,128)} %copy.45.scale_ref), custom_call_target="tpu_custom_call" | custom-call | tf_op jit(solution)/shard_map/pallas_call | solution.py:44
  185.3 37.6 %shard_map.83 = bf16[64,256,128]{2,1,0:T(8,128)(2,1)} custom-call(s32[64]{0:T(128)} %compare_select_fusion.source_ref, bf16[32,256,256]{2,1,0:T(8,128)(2,1)} %copy.46.left_ref, bf16[16,512,128]{2,1,0:T(8,128)(2,1)} %shard_map.82.flux_ref), custom_call_target="tpu_custom_call" | custom-call | tf_op jit(solution)/shard_map/pallas_call | solution.py:88
  223.0 7.4 %all-to-all-start.2 = ((bf16[32,512,128]{2,1,0:T(8,128)(2,1)}), bf16[32,512,128]{2,1,0:T(8,128)(2,1)}, u32[]{:S(2)}, u32[]{:S(2)}) async-start(bf16[32,512,128]{2,1,0:T(8,128)(2,1)} %bitcast.98), calls=%async_computation.2 | async-start | bytes 8388608 | tf_op jit(solution)/shard_map/all_to_all | solution.py:197
  230.3 22.5 %shard_map.84.flux_ref = bf16[16,512,128]{2,1,0:T(8,128)(2,1)} custom-call(bf16[16,512,1024]{2,1,0:T(8,128)(2,1)} %get-tuple-element.9.hi_ref, bf16[16,512,1024]{2,1,0:T(8,128)(2,1)} %get-tuple-element.10.lo_ref, bf16[1024,2048]{1,0:T(8,128)(2,1)} %bitcast.31.rows_ref, bf16[16,512,256]{2,1,0:T(8,128)(2,1)} %bitcast.96, f32[16,512,1]{2,1,0:T(8,128)} %copy.45.scale_ref), custom_call_target="tpu_custom_call" | custom-call | tf_op jit(solution)/shard_map/pallas_call | solution.py:44
  252.9 37.7 %shard_map.85 = bf16[64,256,128]{2,1,0:T(8,128)(2,1)} custom-call(s32[64]{0:T(128)} %compare_select_fusion.source_ref, bf16[32,256,256]{2,1,0:T(8,128)(2,1)} %copy.46.left_ref, bf16[16,512,128]{2,1,0:T(8,128)(2,1)} %shard_map.84.flux_ref), custom_call_target="tpu_custom_call" | custom-call | tf_op jit(solution)/shard_map/pallas_call | solution.py:88
  290.6 7.4 %all-to-all-start.4 = ((bf16[32,512,128]{2,1,0:T(8,128)(2,1)}), bf16[32,512,128]{2,1,0:T(8,128)(2,1)}, u32[]{:S(2)}, u32[]{:S(2)}) async-start(bf16[32,512,128]{2,1,0:T(8,128)(2,1)} %bitcast.99), calls=%async_computation.4 | async-start | bytes 8388608 | tf_op jit(solution)/shard_map/all_to_all | solution.py:197
  298.1 4.6 %fusion.4 = f32[16,256,128]{2,0,1:T(8,128)S(1)} fusion(bf16[64,256,128]{2,1,0:T(8,128)(2,1)} %bitcast.29, s32[64]{0:T(128)S(1)} %sub.24), kind=kOutput, calls=%fused_computation.7 | convolution fusion | flops 67109888 | bytes 6291712 | tf_op jit(solution)/shard_map/bx,xnm->bnm/dot_general | solution.py:200
  302.7 48.1 %all-to-all-done.4 = bf16[32,512,128]{2,1,0:T(8,128)(2,1)} async-done(((bf16[32,512,128]{2,1,0:T(8,128)(2,1)}), bf16[32,512,128]{2,1,0:T(8,128)(2,1)}, u32[]{:S(2)}, u32[]{:S(2)}) %all-to-all-start.4) | async-done | bytes 4194336 | tf_op jit(solution)/shard_map/all_to_all | solution.py:197
  350.8 4.5 %fusion.2 = f32[16,256,128]{2,0,1:T(8,128)S(1)} fusion(bf16[64,256,128]{2,1,0:T(8,128)(2,1)} %bitcast.33, s32[64]{0:T(128)S(1)} %sub.24), kind=kOutput, calls=%fused_computation.5 | convolution fusion | flops 67109888 | bytes 6291712 | tf_op jit(solution)/shard_map/bx,xnm->bnm/dot_general | solution.py:200
  355.6 4.4 %copy.51 = f32[16,256,256]{2,1,0:T(8,128)} copy(f32[16,256,256]{2,0,1:T(8,128)S(1)} %pad_maximum_fusion) | data formatting | bytes 8388608 | tf_op jit(solution)/shard_map/concatenate | solution.py:207
  (56 shorter events, 14.2 us)
Async XLA Ops:
  2.3 7.3 %copy-start.3 = (s32[32,1]{0,1:T(1,128)S(1)}, s32[32,1]{0,1:T(1,128)}, u32[]{:S(2)}) copy-start(s32[32,1]{0,1:T(1,128)} %param.14) | copy-start | bytes 388
  2.3 7.6 %copy-start.4 = (s32[32]{0:T(128)S(1)}, s32[32]{0:T(128)}, u32[]{:S(2)}) copy-start(s32[32]{0:T(128)} %param.15) | copy-start | bytes 388
  2.3 7.9 %collective-permute-start = (f32[512,69]{0,1:T(8,128)S(1)}, f32[512,69]{0,1:T(8,128)S(1)}, u32[]{:S(2)}, u32[]{:S(2)}) collective-permute-start(f32[512,69]{0,1:T(8,128)S(1)} %pad_maximum_fusion.1), channel_id=1, source_target_pairs={{96,0},{0,32},{32,64},{64,96},{97,1},{1,33},{33,65},{65,97},{98,2}... | collective-permute-start | bytes 423944 | tf_op jit(solution)/shard_map/ppermute | solution.py:20
  8.1 48.6 %collective-permute-start.1 = (bf16[512,16,128]{2,1,0:T(8,128)(2,1)}, bf16[512,16,128]{2,1,0:T(8,128)(2,1)}, u32[]{:S(2)}, u32[]{:S(2)}) collective-permute-start(bf16[512,16,128]{2,1,0:T(8,128)(2,1)} %get-tuple-element.17), channel_id=1, source_target_pairs={{96,0},{0,32},{32,64},{64,96},{97,1},{1,33},{33,65},{65,97},{98,2}... | collective-permute-start | bytes 6291464 | tf_op jit(solution)/shard_map/ppermute | solution.py:20
  14.2 48.4 %all-to-all-start = ((f32[32,1,2178]{2,1,0:T(1,128)}), f32[32,1,2178]{2,1,0:T(1,128)S(1)}, u32[]{:S(2)}, u32[]{:S(2)}) async-start(f32[32,1,2178]{2,1,0:T(1,128)} %copy.41), calls=%async_computation | async-start | bytes 589824 | tf_op jit(solution)/shard_map/all_to_all | solution.py:152
  62.6 63.5 %all-to-all-start.1 = ((bf16[32,32,2048]{2,1,0:T(8,128)(2,1)}), bf16[32,32,2048]{2,1,0:T(8,128)(2,1)}, u32[]{:S(2)}, u32[]{:S(2)}) async-start(bf16[32,32,2048]{2,1,0:T(8,128)(2,1)} %bitcast.103), calls=%async_computation.1 | async-start | bytes 8388608 | tf_op jit(solution)/shard_map/all_to_all | solution.py:162
  70.9 6.4 %copy-start = (bf16[512,16,256]{2,1,0:T(8,128)(2,1)S(1)}, bf16[512,16,256]{2,1,0:T(8,128)(2,1)}, u32[]{:S(2)}) copy-start(bf16[512,16,256]{2,1,0:T(8,128)(2,1)} %param.12) | copy-start | bytes 12582916
  70.9 49.2 %collective-permute-start.2 = (bf16[512,16,128]{2,1,0:T(8,128)(2,1)S(1)}, bf16[512,16,128]{2,1,0:T(8,128)(2,1)}, u32[]{:S(2)}, u32[]{:S(2)}) collective-permute-start(bf16[512,16,128]{2,1,0:T(8,128)(2,1)S(1)} %get-tuple-element.12), channel_id=1, source_target_pairs={{96,0},{0,32},{32,64},{64,96},{97,1},{1,33},{33,65},{65,97},{98,2}... | collective-permute-start | bytes 6291464 | tf_op jit(solution)/shard_map/ppermute | solution.py:20
  126.0 7.6 %copy-start.1 = (f32[1024,64]{0,1:T(8,128)S(1)}, f32[1024,64]{0,1:T(8,128)}, u32[]{:S(2)}) copy-start(f32[1024,64]{0,1:T(8,128)} %copy.43) | copy-start | bytes 786436
  126.0 96.9 %all-to-all-start.3 = ((bf16[32,32,2048]{2,1,0:T(8,128)(2,1)}), bf16[32,32,2048]{2,1,0:T(8,128)(2,1)}, u32[]{:S(2)}, u32[]{:S(2)}) async-start(bf16[32,32,2048]{2,1,0:T(8,128)(2,1)} %bitcast.102), calls=%async_computation.3 | async-start | bytes 8388608 | tf_op jit(solution)/shard_map/all_to_all | solution.py:162
  136.0 24.2 %copy-start.2 = (f32[512]{0:T(512)S(1)}, f32[512]{0:T(512)}, u32[]{:S(2)}) copy-start(f32[512]{0:T(512)} %param.13) | copy-start | bytes 6148
  223.0 67.7 %all-to-all-start.2 = ((bf16[32,512,128]{2,1,0:T(8,128)(2,1)}), bf16[32,512,128]{2,1,0:T(8,128)(2,1)}, u32[]{:S(2)}, u32[]{:S(2)}) async-start(bf16[32,512,128]{2,1,0:T(8,128)(2,1)} %bitcast.98), calls=%async_computation.2 | async-start | bytes 8388608 | tf_op jit(solution)/shard_map/all_to_all | solution.py:197
  290.6 60.1 %all-to-all-start.4 = ((bf16[32,512,128]{2,1,0:T(8,128)(2,1)}), bf16[32,512,128]{2,1,0:T(8,128)(2,1)}, u32[]{:S(2)}, u32[]{:S(2)}) async-start(bf16[32,512,128]{2,1,0:T(8,128)(2,1)} %bitcast.99), calls=%async_computation.4 | async-start | bytes 8388608 | tf_op jit(solution)/shard_map/all_to_all | solution.py:197
where the time goes:
time: 364 us; the launch traced here: 360 us
  Pallas kernels  120 us (33%)
  waiting for transfers between devices  112 us (31%)
  starting transfers between devices  42.4 us (12%)
  local copies, waits for them, and re-layouts  32.2 us (9%)
  other arithmetic  29.9 us (8%)
  matrix products  22.8 us (6%)
    pallas_call x2, Pallas kernels, packed_tiles_of(): pl.pallas_call(functools.partial(tile_kernel, tile_count), grid_spec=grid...  75.3 us
    ppermute x3, waiting for transfers between devices, shifted(): return lax.ppermute(block, axis, route)  64.1 us
    all_to_all x2, waiting for transfers between devices, on_device(): lax.all_to_all(packed_tiles.reshape(dom_count, tile_capacity * NP, width)...  48.1 us
    pallas_call x2, Pallas kernels, flux_chunk(): pl.pallas_call(flux_kernel, grid=(q_count,), in_specs=[pl.BlockSpec((1, s...  45.1 us
    reduce_sum x1, other arithmetic, on_device(): weight_sum = jnp.sum(table, axis=2)  24.2 us
    all_to_all x2, starting transfers between devices, on_device(): lax.all_to_all(packed.reshape(dom_count, capacity, Q * width), 'dom', 0,...  15.8 us
    all_to_all x2, starting transfers between devices, on_device(): lax.all_to_all(packed_tiles.reshape(dom_count, tile_capacity * NP, width)...  14.7 us
    dot_general x2, matrix products, on_device(): jnp.dot(placer.astype(bf16), moved_chunks[k].reshape(seg_count, Q * width...  11.8 us
  transfers between devices with their start and end apart: 8, of which 3 were waited for; matrix products, arithmetic and copies ran while one was open for 20% of the time, Pallas kernels for 33%

commit v1 on v0

--- a/solution.py
+++ b/solution.py
@@ -56,38 +56,42 @@
     )(table_hi, table_lo, rows, own, scale)
 
 
-def tile_kernel(tile_count, source_ref, left_ref, flux_ref, out_ref):
-    x = pl.program_id(0)
-    real = source_ref[x] < tile_count
-
-    @pl.when(real)
-    def _():
-        q_count, per_tile, width = flux_ref.shape
-        right = flux_ref[...].reshape(q_count * per_tile, width)
-        out_ref[0] = jnp.dot(left_ref[0], right, preferred_element_type=jnp.float32).astype(jnp.bfloat16)
-
-    @pl.when(jnp.logical_not(real))
-    def _():
-        out_ref[...] = jnp.zeros(out_ref.shape, out_ref.dtype)
+def tile_kernel(tile_count, per_tile, source_ref, left_ref, flux_ref, out_ref):
+    width = out_ref.shape[2]
+
+    def body(x, carry):
+        src = source_ref[x]
+
+        @pl.when(src < tile_count)
+        def _():
+            first = pl.multiple_of(src * per_tile, per_tile)
+            right = flux_ref[:, pl.ds(first, per_tile), :].reshape(-1, width)
+            out_ref[x] = jnp.dot(
+                left_ref[src], right, preferred_element_type=jnp.float32
+            ).astype(jnp.bfloat16)
+
+        @pl.when(src >= tile_count)
+        def _():
+            out_ref[x] = jnp.zeros(out_ref.shape[1:], out_ref.dtype)
+
+        return carry
+
+    lax.fori_loop(0, out_ref.shape[0], body, 0)
 
 
 def packed_tiles_of(source, left, flux, per_tile):
     tile_slots = source.shape[0]
     tile_count, rows, depth = left.shape
-    q_count, slave_count, width = flux.shape
-    last = tile_count - 1
-    grid_spec = pltpu.PrefetchScalarGridSpec(
-        num_scalar_prefetch=1,
-        grid=(tile_slots,),
+    width = flux.shape[2]
+    vmem = pltpu.MemorySpace.VMEM if hasattr(pltpu, "MemorySpace") else pltpu.TPUMemorySpace.VMEM
+    return pl.pallas_call(
+        functools.partial(tile_kernel, tile_count, per_tile),
         in_specs=[
-            pl.BlockSpec((1, rows, depth), lambda x, src: (jnp.minimum(src[x], last), 0, 0)),
-            pl.BlockSpec((q_count, per_tile, width), lambda x, src: (0, jnp.minimum(src[x], last), 0)),
-        ],
-        out_specs=pl.BlockSpec((1, rows, width), lambda x, src: (x, 0, 0)),
-    )
-    return pl.pallas_call(
-        functools.partial(tile_kernel, tile_count),
-        grid_spec=grid_spec,
+            pl.BlockSpec(memory_space=pltpu.SMEM),
+            pl.BlockSpec(memory_space=vmem),
+            pl.BlockSpec(memory_space=vmem),
+        ],
+        out_specs=pl.BlockSpec(memory_space=vmem),
         out_shape=jax.ShapeDtypeStruct((tile_slots, rows, width), jnp.bfloat16),
     )(source, left, flux)
 
@@ -151,17 +155,6 @@
     )
     got_meta = lax.all_to_all(send_meta, "dom", 0, 0, tiled=True)
 
-    got_chunks = []
-    for k in range(SPLIT):
-        packed = jnp.dot(
-            placer.astype(bf16),
-            moved_chunks[k].reshape(seg_count, Q * width),
-            preferred_element_type=f32,
-        ).astype(bf16)
-        got_chunks.append(
-            lax.all_to_all(packed.reshape(dom_count, capacity, Q * width), "dom", 0, 0, tiled=True)
-        )
-
     got_records = got_meta[:, : capacity * rec_cols].reshape(slots, rec_cols)
     got_weights = got_records[:, :wcols].reshape(slots, PAIRS, Q)
     got_owners = got_records[:, wcols:].astype(i32) - 1
@@ -177,8 +170,23 @@
     table_hi = table.astype(bf16)
     table_lo = (table - table_hi.astype(f32)).astype(bf16)
     weight_sum = jnp.sum(table, axis=2)
-    table_hi, table_lo, weight_sum = lax.optimization_barrier((table_hi, table_lo, weight_sum))
+    tables = lax.optimization_barrier((table_hi, table_lo, weight_sum))
+    table_hi, table_lo, weight_sum = tables
     scale = (jnp.transpose(slave_gain[:, None]) + weight_sum)[:, :, None]
+
+    got_chunks = []
+    for k in range(SPLIT):
+        moved = moved_chunks[k]
+        if k == 1:
+            moved, _ = lax.optimization_barrier((moved, tables))
+        packed = jnp.dot(
+            placer.astype(bf16),
+            moved.reshape(seg_count, Q * width),
+            preferred_element_type=f32,
+        ).astype(bf16)
+        got_chunks.append(
+            lax.all_to_all(packed.reshape(dom_count, capacity, Q * width), "dom", 0, 0, tiled=True)
+        )
 
     got_rows = got_meta[:, capacity * rec_cols:].reshape(tile_slots).astype(i32) - 1
     selector = (got_rows[None, :] == jnp.arange(BR, dtype=i32)[:, None]).astype(bf16)

time: 364 us -> 318 us (0.87)
  Pallas kernels: 120 us -> 68.2 us
  blocking collectives: 0 us -> 15.6 us
  starting transfers between devices: 42.4 us -> 32.8 us
  waiting for transfers between devices: 112 us -> 116 us
    pallas_call x2, Pallas kernels: 75.3 us -> 23.2 us  [packed_tiles_of(): pl.pallas_call(functools.partial(tile_kernel, tile_count, per_tile), in_s...]
    all_to_all x2, waiting for transfers between devices: 48.1 us -> 67.1 us  [on_device(): lax.all_to_all(packed_tiles.reshape(dom_count, tile_capacity * NP, width)...]
    ppermute x3, waiting for transfers between devices: 64.1 us -> 48.4 us  [shifted(): return lax.ppermute(block, axis, route)]
    all_to_all x0 -> x1, blocking collectives: none -> 15.6 us  [on_device(): got_meta = lax.all_to_all(send_meta, 'dom', 0, 0, tiled=True)]
    all_to_all x1 -> x0, starting transfers between devices: 8.21 us -> none  [on_device(): got_meta = lax.all_to_all(send_meta, 'dom', 0, 0, tiled=True)]
  transfers between devices with their start and end apart: 8 -> 7, of which waited for: 3 -> 4; matrix products, arithmetic and copies ran while one was open for 20% -> 21% of each run, Pallas kernels for 33% -> 22%
where the time goes in v1:
time: 318 us; the launch traced here: 316 us
  waiting for transfers between devices  116 us (36%)
  Pallas kernels  68.2 us (21%)
  starting transfers between devices  32.8 us (10%)
  local copies, waits for them, and re-layouts  32.3 us (10%)
  other arithmetic  29.9 us (9%)
  matrix products  21.2 us (7%)
  blocking collectives  15.6 us (5%)
    all_to_all x2, waiting for transfers between devices, on_device(): lax.all_to_all(packed_tiles.reshape(dom_count, tile_capacity * NP, width)...  67.1 us
    ppermute x3, waiting for transfers between devices, shifted(): return lax.ppermute(block, axis, route)  48.4 us
    pallas_call x2, Pallas kernels, flux_chunk(): pl.pallas_call(flux_kernel, grid=(q_count,), in_specs=[pl.BlockSpec((1, s...  45.1 us
    reduce_sum x1, other arithmetic, on_device(): weight_sum = jnp.sum(table, axis=2)  24.2 us
    pallas_call x2, Pallas kernels, packed_tiles_of(): pl.pallas_call(functools.partial(tile_kernel, tile_count, per_tile), in_s...  23.2 us
    all_to_all x2, starting transfers between devices, on_device(): lax.all_to_all(packed.reshape(dom_count, capacity, Q * width), 'dom', 0,...  15.7 us
    all_to_all x1, blocking collectives, on_device(): got_meta = lax.all_to_all(send_meta, 'dom', 0, 0, tiled=True)  15.6 us
    all_to_all x2, starting transfers between devices, on_device(): lax.all_to_all(packed_tiles.reshape(dom_count, tile_capacity * NP, width)...  13.5 us
  transfers between devices with their start and end apart: 7, of which 4 were waited for; matrix products, arithmetic and copies ran while one was open for 21% of the time, Pallas kernels for 22%

profile of v1, /device:TPU:32, one launch (start us, length us, event | category | flops | bytes accessed | tf_op | source)
XLA Modules:
  0.0 315.7 jit_solution(14797854775165552157)
XLA Ops:
  3.8 4.3 %fusion.39 = (bf16[512,16,128]{2,1,0:T(8,128)(2,1)}, bf16[512,16,128]{2,1,0:T(8,128)(2,1)S(1)}) fusion(bf16[512,16,256]{2,1,0:T(8,128)(2,1)} %param.8), kind=kLoop, calls=%fused_computation.81 | loop fusion | bytes 8388608 | tf_op jit(solution)/shard_map/slice | solution.py:133
  13.5 15.6 %all_to_all.32 = f32[32,1,2178]{2,1,0:T(1,128)S(1)} all-to-all(f32[32,1,2178]{2,1,0:T(1,128)S(1)} %copy.41), channel_id=1, replica_groups=mesh['body'=4,'dom'=32] {'dom'}, dimensions={0} | all-to-all | bytes 557568 | tf_op jit(solution)/shard_map/all_to_all | solution.py:156
  32.7 24.0 %collective-permute-done.1 = bf16[512,16,128]{2,1,0:T(8,128)(2,1)} collective-permute-done((bf16[512,16,128]{2,1,0:T(8,128)(2,1)}, bf16[512,16,128]{2,1,0:T(8,128)(2,1)}, u32[]{:S(2)}, u32[]{:S(2)}) %collective-permute-start.1) | collective-permute-done | bytes 2097184 | tf_op jit(solution)/shard_map/ppermute | solution.py:20
  56.7 6.0 %convolution_convert_fusion.1 = bf16[1024,2048]{1,0:T(8,128)(2,1)} fusion(bf16[64,8,16,128]{3,2,1,0:T(8,128)(2,1)} %bitcast.43, s32[512]{0:T(512)S(1)} %add.53), kind=kOutput, calls=%fused_computation.11 | convolution fusion | flops 2150105088 | bytes 6293504 | tf_op jit(solution)/shard_map/dot_general | solution.py:182
  62.7 8.3 %all-to-all-start.1 = ((bf16[32,32,2048]{2,1,0:T(8,128)(2,1)}), bf16[32,32,2048]{2,1,0:T(8,128)(2,1)}, u32[]{:S(2)}, u32[]{:S(2)}) async-start(bf16[32,32,2048]{2,1,0:T(8,128)(2,1)} %bitcast.102), calls=%async_computation.1 | async-start | bytes 8388608 | tf_op jit(solution)/shard_map/all_to_all | solution.py:188
  73.1 24.2 %fusion = (f32[16,512]{1,0:T(8,128)S(1)}, bf16[16,512,1024]{2,1,0:T(8,128)(2,1)}, bf16[16,512,1024]{2,1,0:T(8,128)(2,1)}) fusion(f32[16,1024]{1,0:T(8,128)S(1)} %get-tuple-element.25, f32[16,1024]{1,0:T(8,128)S(1)} %get-tuple-element.26, f32[16,1024]{1,0:T(8,128)S(1)} %get-tuple-element.27, f32[16,1024]{1,0:T(8,128)S(1)} %get-tuple-element.24, ...), kind=kLoop, calls=%fused_computation.2 | loop fusion | flops 100655104 | bytes 35946496 | tf_op jit(solution)/shard_map/reduce_sum | solution.py:172
  97.2 24.4 %collective-permute-done.2 = bf16[512,16,128]{2,1,0:T(8,128)(2,1)S(1)} collective-permute-done((bf16[512,16,128]{2,1,0:T(8,128)(2,1)S(1)}, bf16[512,16,128]{2,1,0:T(8,128)(2,1)S(1)}, u32[]{:S(2)}, u32[]{:S(2)}) %collective-permute-start.2) | collective-permute-done | bytes 2097184 | tf_op jit(solution)/shard_map/ppermute | solution.py:20
  121.6 4.4 %convolution_convert_fusion = bf16[1024,2048]{1,0:T(8,128)(2,1)} fusion(bf16[64,8,16,128]{3,2,1,0:T(8,128)(2,1)S(1)} %bitcast.112, s32[512]{0:T(512)S(1)} %add.53), kind=kOutput, calls=%fused_computation.10 | convolution fusion | flops 2150105088 | bytes 6293504 | tf_op jit(solution)/shard_map/dot_general | solution.py:182
  126.0 7.5 %all-to-all-start.3 = ((bf16[32,32,2048]{2,1,0:T(8,128)(2,1)}), bf16[32,32,2048]{2,1,0:T(8,128)(2,1)}, u32[]{:S(2)}, u32[]{:S(2)}) async-start(bf16[32,32,2048]{2,1,0:T(8,128)(2,1)} %bitcast.103), calls=%async_computation.3 | async-start | bytes 8388608 | tf_op jit(solution)/shard_map/all_to_all | solution.py:188
  133.5 5.7 %copy.72 = bf16[512,16,256]{2,0,1:T(8,128)(2,1)} copy(bf16[512,16,256]{2,1,0:T(8,128)(2,1)} %param.12) | data formatting | bytes 8388608 | tf_op args[4]
  139.2 3.9 %copy.42 = bf16[32,256,16,16]{1,3,2,0:T(8,128)(2,1)} copy(bf16[32,256,16,16]{1,2,3,0:T(8,128)(2,1)S(1)} %bitcast.97) | data formatting | bytes 8388608 | tf_op jit(solution)/shard_map/transpose | solution.py:196
  143.1 6.4 %copy.46.left_ref = bf16[32,256,256]{2,1,0:T(8,128)(2,1)} copy(bf16[32,256,256]{1,2,0:T(8,128)(2,1)} %bitcast.100) | data formatting | bytes 8388608 | tf_op jit(solution)/shard_map/reshape | solution.py:198
  150.2 2.7 copy.45.scale_ref
  152.9 22.5 %shard_map.82.flux_ref = bf16[16,512,128]{2,1,0:T(8,128)(2,1)} custom-call(bf16[16,512,1024]{2,1,0:T(8,128)(2,1)} %get-tuple-element.10.hi_ref, bf16[16,512,1024]{2,1,0:T(8,128)(2,1)} %get-tuple-element.11.lo_ref, bf16[1024,2048]{1,0:T(8,128)(2,1)} %bitcast.25.rows_ref, bf16[16,512,256]{2,1,0:T(8,128)(2,1)} %bitcast.95, f32[16,512,1]{2,1,0:T(8,128)} %copy.45.scale_ref), custom_call_target="tpu_custom_call" | custom-call | tf_op jit(solution)/shard_map/pallas_call | solution.py:44
  175.4 11.5 %shard_map.83 = bf16[64,256,128]{2,1,0:T(8,128)(2,1)} custom-call(s32[64]{0:T(128)} %compare_select_fusion.source_ref, bf16[32,256,256]{2,1,0:T(8,128)(2,1)} %copy.46.left_ref, bf16[16,512,128]{2,1,0:T(8,128)(2,1)} %shard_map.82.flux_ref), custom_call_target="tpu_custom_call" | custom-call | tf_op jit(solution)/shard_map/pallas_call | solution.py:87
  186.9 7.4 %all-to-all-start.2 = ((bf16[32,512,128]{2,1,0:T(8,128)(2,1)}), bf16[32,512,128]{2,1,0:T(8,128)(2,1)}, u32[]{:S(2)}, u32[]{:S(2)}) async-start(bf16[32,512,128]{2,1,0:T(8,128)(2,1)} %bitcast.98), calls=%async_computation.2 | async-start | bytes 8388608 | tf_op jit(solution)/shard_map/all_to_all | solution.py:205
  194.4 22.5 %shard_map.84.flux_ref = bf16[16,512,128]{2,1,0:T(8,128)(2,1)} custom-call(bf16[16,512,1024]{2,1,0:T(8,128)(2,1)} %get-tuple-element.10.hi_ref, bf16[16,512,1024]{2,1,0:T(8,128)(2,1)} %get-tuple-element.11.lo_ref, bf16[1024,2048]{1,0:T(8,128)(2,1)} %bitcast.31.rows_ref, bf16[16,512,256]{2,1,0:T(8,128)(2,1)} %bitcast.96, f32[16,512,1]{2,1,0:T(8,128)} %copy.45.scale_ref), custom_call_target="tpu_custom_call" | custom-call | tf_op jit(solution)/shard_map/pallas_call | solution.py:44
  216.9 11.6 %shard_map.85 = bf16[64,256,128]{2,1,0:T(8,128)(2,1)} custom-call(s32[64]{0:T(128)} %compare_select_fusion.source_ref, bf16[32,256,256]{2,1,0:T(8,128)(2,1)} %copy.46.left_ref, bf16[16,512,128]{2,1,0:T(8,128)(2,1)} %shard_map.84.flux_ref), custom_call_target="tpu_custom_call" | custom-call | tf_op jit(solution)/shard_map/pallas_call | solution.py:87
  228.5 19.0 %all-to-all-done.2 = bf16[32,512,128]{2,1,0:T(8,128)(2,1)} async-done(((bf16[32,512,128]{2,1,0:T(8,128)(2,1)}), bf16[32,512,128]{2,1,0:T(8,128)(2,1)}, u32[]{:S(2)}, u32[]{:S(2)}) %all-to-all-start.2) | async-done | bytes 4194336 | tf_op jit(solution)/shard_map/all_to_all | solution.py:205
  247.5 6.1 %all-to-all-start.4 = ((bf16[32,512,128]{2,1,0:T(8,128)(2,1)}), bf16[32,512,128]{2,1,0:T(8,128)(2,1)}, u32[]{:S(2)}, u32[]{:S(2)}) async-start(bf16[32,512,128]{2,1,0:T(8,128)(2,1)} %bitcast.99), calls=%async_computation.4 | async-start | bytes 8388608 | tf_op jit(solution)/shard_map/all_to_all | solution.py:205
  253.7 4.6 %fusion.4 = f32[16,256,128]{2,0,1:T(8,128)S(1)} fusion(bf16[64,256,128]{2,1,0:T(8,128)(2,1)} %bitcast.29, s32[64]{0:T(128)S(1)} %sub.24), kind=kOutput, calls=%fused_computation.7 | convolution fusion | flops 67109888 | bytes 6291712 | tf_op jit(solution)/shard_map/bx,xnm->bnm/dot_general | solution.py:208
  258.3 48.1 %all-to-all-done.4 = bf16[32,512,128]{2,1,0:T(8,128)(2,1)} async-done(((bf16[32,512,128]{2,1,0:T(8,128)(2,1)}), bf16[32,512,128]{2,1,0:T(8,128)(2,1)}, u32[]{:S(2)}, u32[]{:S(2)}) %all-to-all-start.4) | async-done | bytes 4194336 | tf_op jit(solution)/shard_map/all_to_all | solution.py:205
  306.4 4.5 %fusion.2 = f32[16,256,128]{2,0,1:T(8,128)S(1)} fusion(bf16[64,256,128]{2,1,0:T(8,128)(2,1)} %bitcast.33, s32[64]{0:T(128)S(1)} %sub.24), kind=kOutput, calls=%fused_computation.5 | convolution fusion | flops 67109888 | bytes 6291712 | tf_op jit(solution)/shard_map/bx,xnm->bnm/dot_general | solution.py:208
  311.3 4.4 %copy.51 = f32[16,256,256]{2,1,0:T(8,128)} copy(f32[16,256,256]{2,0,1:T(8,128)S(1)} %pad_maximum_fusion) | data formatting | bytes 8388608 | tf_op jit(solution)/shard_map/concatenate | solution.py:215
  (53 shorter events, 15.9 us)
Async XLA Ops:
  2.3 7.3 %copy-start.2 = (s32[32,1]{0,1:T(1,128)S(1)}, s32[32,1]{0,1:T(1,128)}, u32[]{:S(2)}) copy-start(s32[32,1]{0,1:T(1,128)} %param.14) | copy-start | bytes 388
  2.3 7.6 %copy-start.3 = (s32[32]{0:T(128)S(1)}, s32[32]{0:T(128)}, u32[]{:S(2)}) copy-start(s32[32]{0:T(128)} %param.15) | copy-start | bytes 388
  2.3 7.9 %collective-permute-start = (f32[512,69]{0,1:T(8,128)S(1)}, f32[512,69]{0,1:T(8,128)S(1)}, u32[]{:S(2)}, u32[]{:S(2)}) collective-permute-start(f32[512,69]{0,1:T(8,128)S(1)} %pad_maximum_fusion.1), channel_id=1, source_target_pairs={{96,0},{0,32},{32,64},{64,96},{97,1},{1,33},{33,65},{65,97},{98,2}... | collective-permute-start | bytes 423944 | tf_op jit(solution)/shard_map/ppermute | solution.py:20
  8.1 48.6 %collective-permute-start.1 = (bf16[512,16,128]{2,1,0:T(8,128)(2,1)}, bf16[512,16,128]{2,1,0:T(8,128)(2,1)}, u32[]{:S(2)}, u32[]{:S(2)}) collective-permute-start(bf16[512,16,128]{2,1,0:T(8,128)(2,1)} %get-tuple-element.19), channel_id=1, source_target_pairs={{96,0},{0,32},{32,64},{64,96},{97,1},{1,33},{33,65},{65,97},{98,2}... | collective-permute-start | bytes 6291464 | tf_op jit(solution)/shard_map/ppermute | solution.py:20
  62.7 63.3 %all-to-all-start.1 = ((bf16[32,32,2048]{2,1,0:T(8,128)(2,1)}), bf16[32,32,2048]{2,1,0:T(8,128)(2,1)}, u32[]{:S(2)}, u32[]{:S(2)}) async-start(bf16[32,32,2048]{2,1,0:T(8,128)(2,1)} %bitcast.102), calls=%async_computation.1 | async-start | bytes 8388608 | tf_op jit(solution)/shard_map/all_to_all | solution.py:188
  72.5 49.1 %collective-permute-start.2 = (bf16[512,16,128]{2,1,0:T(8,128)(2,1)S(1)}, bf16[512,16,128]{2,1,0:T(8,128)(2,1)S(1)}, u32[]{:S(2)}, u32[]{:S(2)}) collective-permute-start(bf16[512,16,128]{2,1,0:T(8,128)(2,1)S(1)} %get-tuple-element.13), channel_id=1, source_target_pairs={{96,0},{0,32},{32,64},{64,96},{97,1},{1,33},{33,65},{65,97},{98,2}... | collective-permute-start | bytes 6291464 | tf_op jit(solution)/shard_map/ppermute | solution.py:20
  126.0 60.9 %all-to-all-start.3 = ((bf16[32,32,2048]{2,1,0:T(8,128)(2,1)}), bf16[32,32,2048]{2,1,0:T(8,128)(2,1)}, u32[]{:S(2)}, u32[]{:S(2)}) async-start(bf16[32,32,2048]{2,1,0:T(8,128)(2,1)} %bitcast.103), calls=%async_computation.3 | async-start | bytes 8388608 | tf_op jit(solution)/shard_map/all_to_all | solution.py:188
  133.5 5.7 %copy-start = (bf16[512,16,256]{2,1,0:T(8,128)(2,1)S(1)}, bf16[512,16,256]{2,1,0:T(8,128)(2,1)}, u32[]{:S(2)}) copy-start(bf16[512,16,256]{2,1,0:T(8,128)(2,1)} %param.12) | copy-start | bytes 12582916
  143.1 7.1 %copy-start.1 = (f32[512]{0:T(512)S(1)}, f32[512]{0:T(512)}, u32[]{:S(2)}) copy-start(f32[512]{0:T(512)} %param.13) | copy-start | bytes 6148
  186.9 60.6 %all-to-all-start.2 = ((bf16[32,512,128]{2,1,0:T(8,128)(2,1)}), bf16[32,512,128]{2,1,0:T(8,128)(2,1)}, u32[]{:S(2)}, u32[]{:S(2)}) async-start(bf16[32,512,128]{2,1,0:T(8,128)(2,1)} %bitcast.98), calls=%async_computation.2 | async-start | bytes 8388608 | tf_op jit(solution)/shard_map/all_to_all | solution.py:205
  247.5 58.9 %all-to-all-start.4 = ((bf16[32,512,128]{2,1,0:T(8,128)(2,1)}), bf16[32,512,128]{2,1,0:T(8,128)(2,1)}, u32[]{:S(2)}, u32[]{:S(2)}) async-start(bf16[32,512,128]{2,1,0:T(8,128)(2,1)} %bitcast.99), calls=%async_computation.4 | async-start | bytes 8388608 | tf_op jit(solution)/shard_map/all_to_all | solution.py:205

commit v2 on v1

--- a/solution.py
+++ b/solution.py
@@ -94,6 +94,45 @@
         out_specs=pl.BlockSpec(memory_space=vmem),
         out_shape=jax.ShapeDtypeStruct((tile_slots, rows, width), jnp.bfloat16),
     )(source, left, flux)
+
+
+def assemble_kernel(rows_ref, tiles_ref, *refs):
+    out_ref = refs[-1]
+    out_ref[...] = jnp.zeros(out_ref.shape, out_ref.dtype)
+
+    def body(x, carry):
+        row = rows_ref[x]
+
+        @pl.when(row >= 0)
+        def _():
+            out_ref[row] = out_ref[row] + tiles_ref[x].astype(jnp.float32)
+
+        return carry
+
+    lax.fori_loop(0, tiles_ref.shape[0], body, 0)
+
+
+def assemble(rows, tiles, previous, chunk):
+    tile_slots, depth, width = tiles.shape
+    blocks = BR, depth, width
+    specs = [
+        pl.BlockSpec(memory_space=pltpu.SMEM),
+        pl.BlockSpec(tiles.shape, lambda i: (0, 0, 0)),
+    ]
+    operands = [rows, tiles]
+    aliases = {}
+    if previous is not None:
+        specs.append(pl.BlockSpec(memory_space=pl.ANY))
+        operands.append(previous)
+        aliases = {2: 0}
+    return pl.pallas_call(
+        assemble_kernel,
+        grid=(1,),
+        in_specs=specs,
+        out_specs=pl.BlockSpec(blocks, lambda i: (0, 0, chunk)),
+        out_shape=jax.ShapeDtypeStruct((BR, depth, width * SPLIT), jnp.float32),
+        input_output_aliases=aliases,
+    )(*operands)
 
 
 def on_device(
@@ -174,11 +213,22 @@
     table_hi, table_lo, weight_sum = tables
     scale = (jnp.transpose(slave_gain[:, None]) + weight_sum)[:, :, None]
 
+    got_rows = got_meta[:, capacity * rec_cols:].reshape(tile_slots).astype(i32) - 1
+    tile_source = jnp.dot(tile_placer.astype(i32), jnp.arange(1, tile_count + 1, dtype=i32)) - 1
+    tile_source = jnp.where(tile_source < 0, tile_count, tile_source)
+    own = jnp.transpose(slave_basis, (1, 0, 2))
+    left = jnp.transpose(
+        slave_basis.reshape(tile_count, per_tile, Q, NP), (0, 3, 2, 1)
+    ).reshape(tile_count, NP, Q * per_tile)
+
+    staged = (tables, own, left, scale)
     got_chunks = []
     for k in range(SPLIT):
         moved = moved_chunks[k]
         if k == 1:
-            moved, _ = lax.optimization_barrier((moved, tables))
+            moved, staged = lax.optimization_barrier((moved, staged))
+            tables, own, left, scale = staged
+            table_hi, table_lo, weight_sum = tables
         packed = jnp.dot(
             placer.astype(bf16),
             moved.reshape(seg_count, Q * width),
@@ -188,16 +238,7 @@
             lax.all_to_all(packed.reshape(dom_count, capacity, Q * width), "dom", 0, 0, tiled=True)
         )
 
-    got_rows = got_meta[:, capacity * rec_cols:].reshape(tile_slots).astype(i32) - 1
-    selector = (got_rows[None, :] == jnp.arange(BR, dtype=i32)[:, None]).astype(bf16)
-    tile_source = jnp.dot(tile_placer.astype(i32), jnp.arange(1, tile_count + 1, dtype=i32)) - 1
-    tile_source = jnp.where(tile_source < 0, tile_count, tile_source)
-    own = jnp.transpose(slave_basis, (1, 0, 2))
-    left = jnp.transpose(
-        slave_basis.reshape(tile_count, per_tile, Q, NP), (0, 3, 2, 1)
-    ).reshape(tile_count, NP, Q * per_tile)
-
-    parts = []
+    coupling = None
     for k in range(SPLIT):
         rows = got_chunks[k].reshape(slots, Q * width)
         flux = flux_chunk(table_hi, table_lo, rows, own, scale, k)
@@ -205,14 +246,8 @@
         got_tiles = lax.all_to_all(
             packed_tiles.reshape(dom_count, tile_capacity * NP, width), "dom", 0, 0, tiled=True
         )
-        part = jnp.einsum(
-            "bx,xnm->bnm",
-            selector,
-            got_tiles.reshape(tile_slots, NP, width),
-            preferred_element_type=f32,
-        )
-        parts.append(part)
-    return jnp.concatenate(parts, axis=2)
+        coupling = assemble(got_rows, got_tiles.reshape(tile_slots, NP, width), coupling, k)
+    return coupling
 
 
 def solution(mesh):

time: 318 us -> 311 us (0.978)
  blocking collectives: 15.6 us -> 0 us
  Pallas kernels: 68.2 us -> 77.8 us
  matrix products: 21.2 us -> 12.1 us
  starting transfers between devices: 32.8 us -> 39.6 us
  waiting for transfers between devices: 116 us -> 121 us
  local copies, waits for them, and re-layouts: 32.3 us -> 28.2 us
    all_to_all x1 -> x0, blocking collectives: 15.6 us -> none  [on_device(): got_meta = lax.all_to_all(send_meta, 'dom', 0, 0, tiled=True)]
    pallas_call x0 -> x2, Pallas kernels: none -> 9.61 us  [assemble(): pl.pallas_call(assemble_kernel, grid=(1,), in_specs=specs, out_specs=pl.B...]
    all_to_all x2, waiting for transfers between devices: 0.01 us -> 9.24 us  [on_device(): lax.all_to_all(packed.reshape(dom_count, capacity, Q * width), 'dom', 0,...]
    dot_general x2 -> x0, matrix products: 9.1 us -> none  [on_device(): jnp.einsum('bx,xnm->bnm', selector, got_tiles.reshape(tile_slots, NP, wid...]
    optimization_barrier x0 -> x2, local copies, waits for them, and re-layouts: none -> 9.08 us  [on_device(): moved, staged = lax.optimization_barrier((moved, staged))]
    all_to_all x0 -> x1, starting transfers between devices: none -> 8.22 us  [on_device(): got_meta = lax.all_to_all(send_meta, 'dom', 0, 0, tiled=True)]
    reshape x1 -> x0, local copies, waits for them, and re-layouts: 6.43 us -> none  [on_device(): left = jnp.transpose(slave_basis.reshape(tile_count, per_tile, Q, NP), (0...]
    concatenate x1 -> x0, local copies, waits for them, and re-layouts: 4.44 us -> none  [on_device(): return jnp.concatenate(parts, axis=2)]
  transfers between devices with their start and end apart: 7 -> 8, of which waited for: 4 -> 5; matrix products, arithmetic and copies ran while one was open for 21% -> 20% of each run, Pallas kernels for 22% -> 24%
where the time goes in v2:
time: 311 us; the launch traced here: 309 us
  waiting for transfers between devices  121 us (39%)
  Pallas kernels  77.8 us (25%)
  starting transfers between devices  39.6 us (13%)
  other arithmetic  29.8 us (10%)
  local copies, waits for them, and re-layouts  28.2 us (9%)
  matrix products  12.1 us (4%)
    all_to_all x2, waiting for transfers between devices, on_device(): lax.all_to_all(packed_tiles.reshape(dom_count, tile_capacity * NP, width)...  66.8 us
    pallas_call x2, Pallas kernels, flux_chunk(): pl.pallas_call(flux_kernel, grid=(q_count,), in_specs=[pl.BlockSpec((1, s...  45.1 us
    ppermute x3, waiting for transfers between devices, shifted(): return lax.ppermute(block, axis, route)  45 us
    reduce_sum x1, other arithmetic, on_device(): weight_sum = jnp.sum(table, axis=2)  24.4 us
    pallas_call x2, Pallas kernels, packed_tiles_of(): pl.pallas_call(functools.partial(tile_kernel, tile_count, per_tile), in_s...  23.1 us
    all_to_all x2, starting transfers between devices, on_device(): lax.all_to_all(packed.reshape(dom_count, capacity, Q * width), 'dom', 0,...  15.7 us
    all_to_all x2, starting transfers between devices, on_device(): lax.all_to_all(packed_tiles.reshape(dom_count, tile_capacity * NP, width)...  12.1 us
    dot_general x2, matrix products, on_device(): jnp.dot(placer.astype(bf16), moved.reshape(seg_count, Q * width), preferr...  10.3 us
  transfers between devices with their start and end apart: 8, of which 5 were waited for; matrix products, arithmetic and copies ran while one was open for 20% of the time, Pallas kernels for 24%

profile of v2, /device:TPU:32, one launch (start us, length us, event | category | flops | bytes accessed | tf_op | source)
XLA Modules:
  0.0 308.9 jit_solution(8354595648622732578)
XLA Ops:
  3.8 4.3 %fusion.30 = (bf16[512,16,128]{2,1,0:T(8,128)(2,1)}, bf16[512,16,128]{2,1,0:T(8,128)(2,1)S(1)}) fusion(bf16[512,16,256]{2,1,0:T(8,128)(2,1)} %param.8), kind=kLoop, calls=%fused_computation.72 | loop fusion | bytes 8388608 | tf_op jit(solution)/shard_map/slice | solution.py:172
  14.3 8.2 %all-to-all-start = ((f32[32,1,2178]{2,1,0:T(1,128)}), f32[32,1,2178]{2,1,0:T(1,128)S(1)}, u32[]{:S(2)}, u32[]{:S(2)}) async-start(f32[32,1,2178]{2,1,0:T(1,128)} %copy.35), calls=%async_computation | async-start | bytes 589824 | tf_op jit(solution)/shard_map/all_to_all | solution.py:195
  22.5 5.9 %copy.59 = bf16[512,16,256]{2,0,1:T(8,128)(2,1)} copy(bf16[512,16,256]{2,1,0:T(8,128)(2,1)} %param.12) | data formatting | bytes 8388608 | tf_op args[4]
  28.4 3.9 %copy.38 = bf16[32,256,16,16]{1,3,2,0:T(8,128)(2,1)} copy(bf16[32,256,16,16]{1,2,3,0:T(8,128)(2,1)S(1)} %bitcast.93) | data formatting | bytes 8388608 | tf_op jit(solution)/shard_map/transpose | solution.py:220
  35.9 20.9 %collective-permute-done.1 = bf16[512,16,128]{2,1,0:T(8,128)(2,1)} collective-permute-done((bf16[512,16,128]{2,1,0:T(8,128)(2,1)}, bf16[512,16,128]{2,1,0:T(8,128)(2,1)}, u32[]{:S(2)}, u32[]{:S(2)}) %collective-permute-start.1) | collective-permute-done | bytes 2097184 | tf_op jit(solution)/shard_map/ppermute | solution.py:20
  56.8 6.0 %convolution_convert_fusion = bf16[1024,2048]{1,0:T(8,128)(2,1)} fusion(bf16[64,8,16,128]{3,2,1,0:T(8,128)(2,1)} %bitcast.44, s32[512]{0:T(512)S(1)} %add.49), kind=kOutput, calls=%fused_computation.5 | convolution fusion | flops 2150105088 | bytes 6293504 | tf_op jit(solution)/shard_map/dot_general | solution.py:232
  62.7 8.3 %all-to-all-start.3 = ((bf16[32,32,2048]{2,1,0:T(8,128)(2,1)}), bf16[32,32,2048]{2,1,0:T(8,128)(2,1)}, u32[]{:S(2)}, u32[]{:S(2)}) async-start(bf16[32,32,2048]{2,1,0:T(8,128)(2,1)} %bitcast.98), calls=%async_computation.3 | async-start | bytes 8388608 | tf_op jit(solution)/shard_map/all_to_all | solution.py:238
  72.2 24.4 %fusion = (f32[16,512]{1,0:T(8,128)S(1)}, bf16[16,512,1024]{2,1,0:T(8,128)(2,1)}, bf16[16,512,1024]{2,1,0:T(8,128)(2,1)}) fusion(f32[16,1024]{1,0:T(8,128)} %get-tuple-element.35, f32[16,1024]{1,0:T(8,128)} %get-tuple-element.36, f32[16,1024]{1,0:T(8,128)} %get-tuple-element.37, f32[16,1024]{1,0:T(8,128)S(1)} %get-tuple-element.34, ...), kind=kLoop, calls=%fused_computation.2 | loop fusion | flops 100655104 | bytes 35946496 | tf_op jit(solution)/shard_map/reduce_sum | solution.py:211
  96.6 24.1 %collective-permute-done.2 = bf16[512,16,128]{2,1,0:T(8,128)(2,1)S(1)} collective-permute-done((bf16[512,16,128]{2,1,0:T(8,128)(2,1)S(1)}, bf16[512,16,128]{2,1,0:T(8,128)(2,1)S(1)}, u32[]{:S(2)}, u32[]{:S(2)}) %collective-permute-start.2) | collective-permute-done | bytes 2097184 | tf_op jit(solution)/shard_map/ppermute | solution.py:20
  120.8 4.3 %convolution_convert_fusion.1 = bf16[1024,2048]{1,0:T(8,128)(2,1)} fusion(bf16[64,8,16,128]{3,2,1,0:T(8,128)(2,1)S(1)} %bitcast.108, s32[512]{0:T(512)S(1)} %add.49), kind=kOutput, calls=%fused_computation.6 | convolution fusion | flops 2150105088 | bytes 6293504 | tf_op jit(solution)/shard_map/dot_general | solution.py:232
  125.1 7.4 %all-to-all-start.1 = ((bf16[32,32,2048]{2,1,0:T(8,128)(2,1)}), bf16[32,32,2048]{2,1,0:T(8,128)(2,1)}, u32[]{:S(2)}, u32[]{:S(2)}) async-start(bf16[32,32,2048]{2,1,0:T(8,128)(2,1)} %bitcast.99), calls=%async_computation.1 | async-start | bytes 8388608 | tf_op jit(solution)/shard_map/all_to_all | solution.py:238
  133.2 6.4 %copy.40.left_ref = bf16[32,256,256]{2,1,0:T(8,128)(2,1)} copy(bf16[32,256,256]{1,2,0:T(8,128)(2,1)} %bitcast.94) | data formatting | bytes 8388608 | tf_op jit(solution)/shard_map/optimization_barrier | solution.py:229
  139.7 2.7 copy.39.scale_ref
  142.3 22.5 %shard_map.84.flux_ref = bf16[16,512,128]{2,1,0:T(8,128)(2,1)} custom-call(bf16[16,512,1024]{2,1,0:T(8,128)(2,1)} %get-tuple-element.20.hi_ref, bf16[16,512,1024]{2,1,0:T(8,128)(2,1)} %get-tuple-element.21.lo_ref, bf16[1024,2048]{1,0:T(8,128)(2,1)} %bitcast.30.rows_ref, bf16[16,512,256]{2,1,0:T(8,128)(2,1)} %bitcast.91, f32[16,512,1]{2,1,0:T(8,128)} %copy.39.scale_ref), custom_call_target="tpu_custom_call" | custom-call | tf_op jit(solution)/shard_map/pallas_call | solution.py:44
  164.8 11.6 %shard_map.85 = bf16[64,256,128]{2,1,0:T(8,128)(2,1)} custom-call(s32[64]{0:T(128)} %compare_select_fusion.source_ref, bf16[32,256,256]{2,1,0:T(8,128)(2,1)} %copy.40.left_ref, bf16[16,512,128]{2,1,0:T(8,128)(2,1)} %shard_map.84.flux_ref), custom_call_target="tpu_custom_call" | custom-call | tf_op jit(solution)/shard_map/pallas_call | solution.py:87
  176.5 9.2 %all-to-all-done.1 = bf16[32,32,2048]{2,1,0:T(8,128)(2,1)} async-done(((bf16[32,32,2048]{2,1,0:T(8,128)(2,1)}), bf16[32,32,2048]{2,1,0:T(8,128)(2,1)}, u32[]{:S(2)}, u32[]{:S(2)}) %all-to-all-start.1) | async-done | bytes 4194336 | tf_op jit(solution)/shard_map/all_to_all | solution.py:238
  185.7 6.0 %all-to-all-start.4 = ((bf16[32,512,128]{2,1,0:T(8,128)(2,1)}), bf16[32,512,128]{2,1,0:T(8,128)(2,1)}, u32[]{:S(2)}, u32[]{:S(2)}) async-start(bf16[32,512,128]{2,1,0:T(8,128)(2,1)} %bitcast.95), calls=%async_computation.4 | async-start | bytes 8388608 | tf_op jit(solution)/shard_map/all_to_all | solution.py:246
  191.8 22.6 %shard_map.82.flux_ref = bf16[16,512,128]{2,1,0:T(8,128)(2,1)} custom-call(bf16[16,512,1024]{2,1,0:T(8,128)(2,1)} %get-tuple-element.20.hi_ref, bf16[16,512,1024]{2,1,0:T(8,128)(2,1)} %get-tuple-element.21.lo_ref, bf16[1024,2048]{1,0:T(8,128)(2,1)} %bitcast.26.rows_ref, bf16[16,512,256]{2,1,0:T(8,128)(2,1)} %bitcast.92, f32[16,512,1]{2,1,0:T(8,128)} %copy.39.scale_ref), custom_call_target="tpu_custom_call" | custom-call | tf_op jit(solution)/shard_map/pallas_call | solution.py:44
  214.3 11.5 %shard_map.83 = bf16[64,256,128]{2,1,0:T(8,128)(2,1)} custom-call(s32[64]{0:T(128)} %compare_select_fusion.source_ref, bf16[32,256,256]{2,1,0:T(8,128)(2,1)} %copy.40.left_ref, bf16[16,512,128]{2,1,0:T(8,128)(2,1)} %shard_map.82.flux_ref), custom_call_target="tpu_custom_call" | custom-call | tf_op jit(solution)/shard_map/pallas_call | solution.py:87
  225.8 19.1 %all-to-all-done.4 = bf16[32,512,128]{2,1,0:T(8,128)(2,1)} async-done(((bf16[32,512,128]{2,1,0:T(8,128)(2,1)}), bf16[32,512,128]{2,1,0:T(8,128)(2,1)}, u32[]{:S(2)}, u32[]{:S(2)}) %all-to-all-start.4) | async-done | bytes 4194336 | tf_op jit(solution)/shard_map/all_to_all | solution.py:246
  244.9 6.0 %all-to-all-start.2 = ((bf16[32,512,128]{2,1,0:T(8,128)(2,1)}), bf16[32,512,128]{2,1,0:T(8,128)(2,1)}, u32[]{:S(2)}, u32[]{:S(2)}) async-start(bf16[32,512,128]{2,1,0:T(8,128)(2,1)} %bitcast.96), calls=%async_computation.2 | async-start | bytes 8388608 | tf_op jit(solution)/shard_map/all_to_all | solution.py:246
  251.6 4.8 %shard_map.86.refs_0_ = f32[16,256,256]{2,1,0:T(8,128)} custom-call(s32[64]{0:T(128)} %sub.24.rows_ref, bf16[64,256,128]{2,1,0:T(8,128)(2,1)} %bitcast.32.tiles_ref), custom_call_target="tpu_custom_call" | custom-call | tf_op jit(solution)/shard_map/pallas_call | solution.py:128
  256.4 47.7 %all-to-all-done.2 = bf16[32,512,128]{2,1,0:T(8,128)(2,1)} async-done(((bf16[32,512,128]{2,1,0:T(8,128)(2,1)}), bf16[32,512,128]{2,1,0:T(8,128)(2,1)}, u32[]{:S(2)}, u32[]{:S(2)}) %all-to-all-start.2) | async-done | bytes 4194336 | tf_op jit(solution)/shard_map/all_to_all | solution.py:246
  304.1 4.8 %shard_map.87 = f32[16,256,256]{2,1,0:T(8,128)} custom-call(s32[64]{0:T(128)} %sub.24.rows_ref, bf16[64,256,128]{2,1,0:T(8,128)(2,1)} %bitcast.28.tiles_ref, f32[16,256,256]{2,1,0:T(8,128)} %shard_map.86.refs_0_), custom_call_target="tpu_custom_call", output_to_operand_aliasing={{}: (2, {})} | custom-call | tf_op jit(solution)/shard_map/pallas_call | solution.py:128
  (52 shorter events, 15.9 us)
Async XLA Ops:
  2.3 7.4 %copy-start.2 = (s32[32,1]{0,1:T(1,128)S(1)}, s32[32,1]{0,1:T(1,128)}, u32[]{:S(2)}) copy-start(s32[32,1]{0,1:T(1,128)} %param.14) | copy-start | bytes 388
  2.3 7.7 %copy-start.3 = (s32[32]{0:T(128)S(1)}, s32[32]{0:T(128)}, u32[]{:S(2)}) copy-start(s32[32]{0:T(128)} %param.15) | copy-start | bytes 388
  2.3 7.9 %collective-permute-start = (f32[512,69]{0,1:T(8,128)S(1)}, f32[512,69]{0,1:T(8,128)S(1)}, u32[]{:S(2)}, u32[]{:S(2)}) collective-permute-start(f32[512,69]{0,1:T(8,128)S(1)} %pad_maximum_fusion), channel_id=1, source_target_pairs={{96,0},{0,32},{32,64},{64,96},{97,1},{1,33},{33,65},{65,97},{98,2}... | collective-permute-start | bytes 423944 | tf_op jit(solution)/shard_map/ppermute | solution.py:20
  8.1 48.6 %collective-permute-start.1 = (bf16[512,16,128]{2,1,0:T(8,128)(2,1)}, bf16[512,16,128]{2,1,0:T(8,128)(2,1)}, u32[]{:S(2)}, u32[]{:S(2)}) collective-permute-start(bf16[512,16,128]{2,1,0:T(8,128)(2,1)} %get-tuple-element.29), channel_id=1, source_target_pairs={{96,0},{0,32},{32,64},{64,96},{97,1},{1,33},{33,65},{65,97},{98,2}... | collective-permute-start | bytes 6291464 | tf_op jit(solution)/shard_map/ppermute | solution.py:20
  14.3 18.0 %all-to-all-start = ((f32[32,1,2178]{2,1,0:T(1,128)}), f32[32,1,2178]{2,1,0:T(1,128)S(1)}, u32[]{:S(2)}, u32[]{:S(2)}) async-start(f32[32,1,2178]{2,1,0:T(1,128)} %copy.35), calls=%async_computation | async-start | bytes 589824 | tf_op jit(solution)/shard_map/all_to_all | solution.py:195
  22.5 5.9 %copy-start = (bf16[512,16,256]{2,1,0:T(8,128)(2,1)S(1)}, bf16[512,16,256]{2,1,0:T(8,128)(2,1)}, u32[]{:S(2)}) copy-start(bf16[512,16,256]{2,1,0:T(8,128)(2,1)} %param.12) | copy-start | bytes 12582916
  62.7 62.4 %all-to-all-start.3 = ((bf16[32,32,2048]{2,1,0:T(8,128)(2,1)}), bf16[32,32,2048]{2,1,0:T(8,128)(2,1)}, u32[]{:S(2)}, u32[]{:S(2)}) async-start(bf16[32,32,2048]{2,1,0:T(8,128)(2,1)} %bitcast.98), calls=%async_computation.3 | async-start | bytes 8388608 | tf_op jit(solution)/shard_map/all_to_all | solution.py:238
  71.6 49.2 %collective-permute-start.2 = (bf16[512,16,128]{2,1,0:T(8,128)(2,1)S(1)}, bf16[512,16,128]{2,1,0:T(8,128)(2,1)S(1)}, u32[]{:S(2)}, u32[]{:S(2)}) collective-permute-start(bf16[512,16,128]{2,1,0:T(8,128)(2,1)S(1)} %get-tuple-element.15), channel_id=1, source_target_pairs={{96,0},{0,32},{32,64},{64,96},{97,1},{1,33},{33,65},{65,97},{98,2}... | collective-permute-start | bytes 6291464 | tf_op jit(solution)/shard_map/ppermute | solution.py:20
  72.2 24.4 %copy-start.1 = (f32[512]{0:T(512)S(1)}, f32[512]{0:T(512)}, u32[]{:S(2)}) copy-start(f32[512]{0:T(512)} %param.13) | copy-start | bytes 6148
  125.1 60.6 %all-to-all-start.1 = ((bf16[32,32,2048]{2,1,0:T(8,128)(2,1)}), bf16[32,32,2048]{2,1,0:T(8,128)(2,1)}, u32[]{:S(2)}, u32[]{:S(2)}) async-start(bf16[32,32,2048]{2,1,0:T(8,128)(2,1)} %bitcast.99), calls=%async_computation.1 | async-start | bytes 8388608 | tf_op jit(solution)/shard_map/all_to_all | solution.py:238
  185.7 59.2 %all-to-all-start.4 = ((bf16[32,512,128]{2,1,0:T(8,128)(2,1)}), bf16[32,512,128]{2,1,0:T(8,128)(2,1)}, u32[]{:S(2)}, u32[]{:S(2)}) async-start(bf16[32,512,128]{2,1,0:T(8,128)(2,1)} %bitcast.95), calls=%async_computation.4 | async-start | bytes 8388608 | tf_op jit(solution)/shard_map/all_to_all | solution.py:246
  244.9 59.2 %all-to-all-start.2 = ((bf16[32,512,128]{2,1,0:T(8,128)(2,1)}), bf16[32,512,128]{2,1,0:T(8,128)(2,1)}, u32[]{:S(2)}, u32[]{:S(2)}) async-start(bf16[32,512,128]{2,1,0:T(8,128)(2,1)} %bitcast.96), calls=%async_computation.2 | async-start | bytes 8388608 | tf_op jit(solution)/shard_map/all_to_all | solution.py:246

commit v3 on v2

--- a/solution.py
+++ b/solution.py
@@ -167,12 +167,19 @@
         axis=1,
     )
     moved_meta = shifted(meta, "body", 1)
+    hops = lax.axis_size("body") - 1
+    back_rows = seg_count * 3 // 16
+    front_rows = seg_count - back_rows
     moved_chunks = []
     for k in range(SPLIT):
         piece = master_basis[:, :, k * width:(k + 1) * width]
         if moved_chunks:
             piece, _ = lax.optimization_barrier((piece, moved_chunks[-1]))
-        moved_chunks.append(shifted(piece, "body", 1))
+        front = shifted(piece[:front_rows], "body", 1)
+        back = piece[front_rows:]
+        for _ in range(hops):
+            back = shifted(back, "body", -1)
+        moved_chunks.append((front, back))
 
     moved_dest = moved_meta[:, wcols].astype(i32)
     slot = slot_of(moved_dest, dom_count, capacity)
@@ -229,11 +236,18 @@
             moved, staged = lax.optimization_barrier((moved, staged))
             tables, own, left, scale = staged
             table_hi, table_lo, weight_sum = tables
+        front, back = moved
         packed = jnp.dot(
-            placer.astype(bf16),
-            moved.reshape(seg_count, Q * width),
+            placer[:, :front_rows].astype(bf16),
+            front.reshape(front_rows, Q * width),
             preferred_element_type=f32,
-        ).astype(bf16)
+        )
+        packed = packed + jnp.dot(
+            placer[:, front_rows:].astype(bf16),
+            back.reshape(back_rows, Q * width),
+            preferred_element_type=f32,
+        )
+        packed = packed.astype(bf16)
         got_chunks.append(
             lax.all_to_all(packed.reshape(dom_count, capacity, Q * width), "dom", 0, 0, tiled=True)
         )

time: 311 us -> 322 us (1.035)
  starting transfers between devices: 39.6 us -> 51.6 us
  waiting for transfers between devices: 121 us -> 111 us
  matrix products: 12.1 us -> 16.4 us
    ppermute x3 -> x9, waiting for transfers between devices: 45 us -> 14.1 us  [shifted(): return lax.ppermute(block, axis, route)]
    all_to_all x2, waiting for transfers between devices: 9.24 us -> 30.4 us  [on_device(): lax.all_to_all(packed.reshape(dom_count, capacity, Q * width), 'dom', 0,...]
    ppermute x3 -> x9, starting transfers between devices: 3.62 us -> 17.7 us  [shifted(): return lax.ppermute(block, axis, route)]
    slice x1 -> x5, local copies, waits for them, and re-layouts: 0.22 us -> 5.66 us  [the longest x2 4.39 us: on_device(): front = shifted(piece[:front_rows], 'body', 1)]
    dot_general x2 -> x4, matrix products: 10.3 us -> 14.5 us  [the longest x2 7.94 us: on_device(): jnp.dot(placer[:, :front_rows].astype(bf16), front.reshape(front_rows, Q...]
  transfers between devices with their start and end apart: 8 -> 14, of which waited for: 5 -> 7; matrix products, arithmetic and copies ran while one was open for 20% -> 23% of each run, Pallas kernels for 24% -> 23%
where the time goes in v3:
time: 322 us; the launch traced here: 320 us
  waiting for transfers between devices  111 us (34%)
  Pallas kernels  77.8 us (24%)
  starting transfers between devices  51.6 us (16%)
  other arithmetic  32 us (10%)
  local copies, waits for them, and re-layouts  30.7 us (10%)
  matrix products  16.4 us (5%)
    all_to_all x2, waiting for transfers between devices, on_device(): lax.all_to_all(packed_tiles.reshape(dom_count, tile_capacity * NP, width)...  66.8 us
    pallas_call x2, Pallas kernels, flux_chunk(): pl.pallas_call(flux_kernel, grid=(q_count,), in_specs=[pl.BlockSpec((1, s...  45 us
    all_to_all x2, waiting for transfers between devices, on_device(): lax.all_to_all(packed.reshape(dom_count, capacity, Q * width), 'dom', 0,...  30.4 us
    reduce_sum x1, other arithmetic, on_device(): weight_sum = jnp.sum(table, axis=2)  24.4 us
    pallas_call x2, Pallas kernels, packed_tiles_of(): pl.pallas_call(functools.partial(tile_kernel, tile_count, per_tile), in_s...  23.2 us
    ppermute x9, starting transfers between devices, shifted(): return lax.ppermute(block, axis, route)  17.7 us
    ppermute x9, waiting for transfers between devices, shifted(): return lax.ppermute(block, axis, route)  14.1 us
    all_to_all x2, starting transfers between devices, on_device(): lax.all_to_all(packed.reshape(dom_count, capacity, Q * width), 'dom', 0,...  13.6 us
  transfers between devices with their start and end apart: 14, of which 7 were waited for; matrix products, arithmetic and copies ran while one was open for 23% of the time, Pallas kernels for 23%

profile of v3, /device:TPU:32, one launch (start us, length us, event | category | flops | bytes accessed | tf_op | source)
XLA Modules:
  0.0 320.2 jit_solution(12311886560084359598)
XLA Ops:
  14.5 8.2 %all-to-all-start = ((f32[32,1,2178]{2,1,0:T(1,128)}), f32[32,1,2178]{2,1,0:T(1,128)S(1)}, u32[]{:S(2)}, u32[]{:S(2)}) async-start(f32[32,1,2178]{2,1,0:T(1,128)} %copy.35), calls=%async_computation | async-start | bytes 589824 | tf_op jit(solution)/shard_map/all_to_all | solution.py:202
  29.1 3.9 %copy.38 = bf16[32,256,16,16]{1,3,2,0:T(8,128)(2,1)} copy(bf16[32,256,16,16]{1,2,3,0:T(8,128)(2,1)S(1)} %bitcast.103) | data formatting | bytes 8388608 | tf_op jit(solution)/shard_map/transpose | solution.py:227
  40.9 5.3 %collective-permute-done.3 = bf16[96,16,128]{2,1,0:T(8,128)(2,1)} collective-permute-done((bf16[96,16,128]{2,1,0:T(8,128)(2,1)}, bf16[96,16,128]{2,1,0:T(8,128)(2,1)}, u32[]{:S(2)}, u32[]{:S(2)}) %collective-permute-start.3) | collective-permute-done | bytes 393248 | tf_op jit(solution)/shard_map/ppermute | solution.py:20
  46.2 3.7 %collective-permute-start.4 = (bf16[96,16,128]{2,1,0:T(8,128)(2,1)}, bf16[96,16,128]{2,1,0:T(8,128)(2,1)S(1)}, u32[]{:S(2)}, u32[]{:S(2)}) collective-permute-start(bf16[96,16,128]{2,1,0:T(8,128)(2,1)} %collective-permute-done.3), channel_id=1, source_target_pairs={{32,0},{64,32},{96,64},{0,96},{33,1},{65,33},{97,65},{1,97},{34,2}... | collective-permute-start | bytes 1179656 | tf_op jit(solution)/shard_map/ppermute | solution.py:20
  52.2 5.8 %collective-permute-done.4 = bf16[96,16,128]{2,1,0:T(8,128)(2,1)S(1)} collective-permute-done((bf16[96,16,128]{2,1,0:T(8,128)(2,1)}, bf16[96,16,128]{2,1,0:T(8,128)(2,1)S(1)}, u32[]{:S(2)}, u32[]{:S(2)}) %collective-permute-start.4) | collective-permute-done | bytes 393248 | tf_op jit(solution)/shard_map/ppermute | solution.py:20
  63.1 4.0 %fusion.2 = f32[1024,2048]{1,0:T(8,128)S(1)} fusion(bf16[52,8,16,128]{3,2,1,0:T(8,128)(2,1)} %bitcast.46, pred[1024,512]{1,0:T(32,128)(4,1)S(1)} %copy-done.3), kind=kOutput, calls=%fused_computation.12 | convolution fusion | flops 1744830464 | bytes 10616832 | tf_op jit(solution)/shard_map/dot_general | solution.py:240
  70.0 3.7 %collective-permute-start.7 = (bf16[96,16,128]{2,1,0:T(8,128)(2,1)S(1)}, bf16[96,16,128]{2,1,0:T(8,128)(2,1)}, u32[]{:S(2)}, u32[]{:S(2)}) collective-permute-start(bf16[96,16,128]{2,1,0:T(8,128)(2,1)S(1)} %collective-permute-done.6), channel_id=1, source_target_pairs={{32,0},{64,32},{96,64},{0,96},{33,1},{65,33},{97,65},{1,97},{34,2}... | collective-permute-start | bytes 1179656 | tf_op jit(solution)/shard_map/ppermute | solution.py:20
  77.0 7.6 %all-to-all-start.3 = ((bf16[32,32,2048]{2,1,0:T(8,128)(2,1)}), bf16[32,32,2048]{2,1,0:T(8,128)(2,1)}, u32[]{:S(2)}, u32[]{:S(2)}) async-start(bf16[32,32,2048]{2,1,0:T(8,128)(2,1)} %bitcast.101), calls=%async_computation.3 | async-start | bytes 8388608 | tf_op jit(solution)/shard_map/all_to_all | solution.py:252
  84.7 24.4 %fusion = (f32[16,512]{1,0:T(8,128)S(1)}, bf16[16,512,1024]{2,1,0:T(8,128)(2,1)}, bf16[16,512,1024]{2,1,0:T(8,128)(2,1)}) fusion(f32[16,1024]{1,0:T(8,128)S(1)} %copy-done.6, f32[16,1024]{1,0:T(8,128)S(1)} %copy-done.7, f32[16,1024]{1,0:T(8,128)} %get-tuple-element.37, f32[16,1024]{1,0:T(8,128)S(1)} %get-tuple-element.34, pred[512,1024]{1,0:T(8,128)(4,1)S(1)} %copy-done.1, ...), kind=kLoop, calls=%fused_computation.2 | loop fusion | flops 100655104 | bytes 35946496 | tf_op jit(solution)/shard_map/reduce_sum | solution.py:218
  109.2 4.0 %fusion.5 = f32[1024,2048]{1,0:T(8,128)S(1)} fusion(bf16[52,8,16,128]{3,2,1,0:T(8,128)(2,1)} %bitcast.42, pred[1024,512]{1,0:T(32,128)(4,1)S(1)} %copy-done.4), kind=kOutput, calls=%fused_computation.15 | convolution fusion | flops 1744830464 | bytes 10616832 | tf_op jit(solution)/shard_map/dot_general | solution.py:240
  116.5 21.3 %all-to-all-done.3 = bf16[32,32,2048]{2,1,0:T(8,128)(2,1)} async-done(((bf16[32,32,2048]{2,1,0:T(8,128)(2,1)}), bf16[32,32,2048]{2,1,0:T(8,128)(2,1)}, u32[]{:S(2)}, u32[]{:S(2)}) %all-to-all-start.3) | async-done | bytes 4194336 | tf_op jit(solution)/shard_map/all_to_all | solution.py:252
  137.7 6.0 %all-to-all-start.1 = ((bf16[32,32,2048]{2,1,0:T(8,128)(2,1)}), bf16[32,32,2048]{2,1,0:T(8,128)(2,1)}, u32[]{:S(2)}, u32[]{:S(2)}) async-start(bf16[32,32,2048]{2,1,0:T(8,128)(2,1)} %bitcast.102), calls=%async_computation.1 | async-start | bytes 8388608 | tf_op jit(solution)/shard_map/all_to_all | solution.py:252
  144.5 6.5 %copy.40.left_ref = bf16[32,256,256]{2,1,0:T(8,128)(2,1)} copy(bf16[32,256,256]{1,2,0:T(8,128)(2,1)} %bitcast.104) | data formatting | bytes 8388608 | tf_op jit(solution)/shard_map/optimization_barrier | solution.py:236
  153.7 22.5 %shard_map.84.flux_ref = bf16[16,512,128]{2,1,0:T(8,128)(2,1)} custom-call(bf16[16,512,1024]{2,1,0:T(8,128)(2,1)} %get-tuple-element.21.hi_ref, bf16[16,512,1024]{2,1,0:T(8,128)(2,1)} %get-tuple-element.22.lo_ref, bf16[1024,2048]{1,0:T(8,128)(2,1)} %bitcast.30.rows_ref, bf16[16,512,256]{2,1,0:T(8,128)(2,1)} %bitcast.99, f32[16,512,1]{2,1,0:T(8,128)} %copy.39.scale_ref), custom_call_target="tpu_custom_call" | custom-call | tf_op jit(solution)/shard_map/pallas_call | solution.py:44
  176.2 11.6 %shard_map.85 = bf16[64,256,128]{2,1,0:T(8,128)(2,1)} custom-call(s32[64]{0:T(128)} %compare_select_fusion.source_ref, bf16[32,256,256]{2,1,0:T(8,128)(2,1)} %copy.40.left_ref, bf16[16,512,128]{2,1,0:T(8,128)(2,1)} %shard_map.84.flux_ref), custom_call_target="tpu_custom_call" | custom-call | tf_op jit(solution)/shard_map/pallas_call | solution.py:87
  187.8 9.1 %all-to-all-done.1 = bf16[32,32,2048]{2,1,0:T(8,128)(2,1)} async-done(((bf16[32,32,2048]{2,1,0:T(8,128)(2,1)}), bf16[32,32,2048]{2,1,0:T(8,128)(2,1)}, u32[]{:S(2)}, u32[]{:S(2)}) %all-to-all-start.1) | async-done | bytes 4194336 | tf_op jit(solution)/shard_map/all_to_all | solution.py:252
  196.9 6.0 %all-to-all-start.4 = ((bf16[32,512,128]{2,1,0:T(8,128)(2,1)}), bf16[32,512,128]{2,1,0:T(8,128)(2,1)}, u32[]{:S(2)}, u32[]{:S(2)}) async-start(bf16[32,512,128]{2,1,0:T(8,128)(2,1)} %bitcast.105), calls=%async_computation.4 | async-start | bytes 8388608 | tf_op jit(solution)/shard_map/all_to_all | solution.py:260
  203.0 22.5 %shard_map.82.flux_ref = bf16[16,512,128]{2,1,0:T(8,128)(2,1)} custom-call(bf16[16,512,1024]{2,1,0:T(8,128)(2,1)} %get-tuple-element.21.hi_ref, bf16[16,512,1024]{2,1,0:T(8,128)(2,1)} %get-tuple-element.22.lo_ref, bf16[1024,2048]{1,0:T(8,128)(2,1)} %bitcast.26.rows_ref, bf16[16,512,256]{2,1,0:T(8,128)(2,1)} %bitcast.100, f32[16,512,1]{2,1,0:T(8,128)} %copy.39.scale_ref), custom_call_target="tpu_custom_call" | custom-call | tf_op jit(solution)/shard_map/pallas_call | solution.py:44
  225.5 11.5 %shard_map.83 = bf16[64,256,128]{2,1,0:T(8,128)(2,1)} custom-call(s32[64]{0:T(128)} %compare_select_fusion.source_ref, bf16[32,256,256]{2,1,0:T(8,128)(2,1)} %copy.40.left_ref, bf16[16,512,128]{2,1,0:T(8,128)(2,1)} %shard_map.82.flux_ref), custom_call_target="tpu_custom_call" | custom-call | tf_op jit(solution)/shard_map/pallas_call | solution.py:87
  237.1 19.1 %all-to-all-done.4 = bf16[32,512,128]{2,1,0:T(8,128)(2,1)} async-done(((bf16[32,512,128]{2,1,0:T(8,128)(2,1)}), bf16[32,512,128]{2,1,0:T(8,128)(2,1)}, u32[]{:S(2)}, u32[]{:S(2)}) %all-to-all-start.4) | async-done | bytes 4194336 | tf_op jit(solution)/shard_map/all_to_all | solution.py:260
  256.2 6.0 %all-to-all-start.2 = ((bf16[32,512,128]{2,1,0:T(8,128)(2,1)}), bf16[32,512,128]{2,1,0:T(8,128)(2,1)}, u32[]{:S(2)}, u32[]{:S(2)}) async-start(bf16[32,512,128]{2,1,0:T(8,128)(2,1)} %bitcast.106), calls=%async_computation.2 | async-start | bytes 8388608 | tf_op jit(solution)/shard_map/all_to_all | solution.py:260
  262.9 4.8 %shard_map.86.refs_0_ = f32[16,256,256]{2,1,0:T(8,128)} custom-call(s32[64]{0:T(128)} %sub.24.rows_ref, bf16[64,256,128]{2,1,0:T(8,128)(2,1)} %bitcast.32.tiles_ref), custom_call_target="tpu_custom_call" | custom-call | tf_op jit(solution)/shard_map/pallas_call | solution.py:128
  267.7 47.6 %all-to-all-done.2 = bf16[32,512,128]{2,1,0:T(8,128)(2,1)} async-done(((bf16[32,512,128]{2,1,0:T(8,128)(2,1)}), bf16[32,512,128]{2,1,0:T(8,128)(2,1)}, u32[]{:S(2)}, u32[]{:S(2)}) %all-to-all-start.2) | async-done | bytes 4194336 | tf_op jit(solution)/shard_map/all_to_all | solution.py:260
  315.4 4.8 %shard_map.87 = f32[16,256,256]{2,1,0:T(8,128)} custom-call(s32[64]{0:T(128)} %sub.24.rows_ref, bf16[64,256,128]{2,1,0:T(8,128)(2,1)} %bitcast.28.tiles_ref, f32[16,256,256]{2,1,0:T(8,128)} %shard_map.86.refs_0_), custom_call_target="tpu_custom_call", output_to_operand_aliasing={{}: (2, {})} | custom-call | tf_op jit(solution)/shard_map/pallas_call | solution.py:128
  (85 shorter events, 49.7 us)
Async XLA Ops:
  0.0 9.9 %copy-start.9 = (s32[32,1]{0,1:T(1,128)S(1)}, s32[32,1]{0,1:T(1,128)}, u32[]{:S(2)}) copy-start(s32[32,1]{0,1:T(1,128)} %param.14) | copy-start | bytes 388
  0.0 10.2 %copy-start.10 = (s32[32]{0:T(128)S(1)}, s32[32]{0:T(128)}, u32[]{:S(2)}) copy-start(s32[32]{0:T(128)} %param.15) | copy-start | bytes 388
  2.3 8.2 %collective-permute-start = (f32[512,69]{0,1:T(8,128)S(1)}, f32[512,69]{0,1:T(8,128)S(1)}, u32[]{:S(2)}, u32[]{:S(2)}) collective-permute-start(f32[512,69]{0,1:T(8,128)S(1)} %pad_maximum_fusion), channel_id=1, source_target_pairs={{96,0},{0,32},{32,64},{64,96},{97,1},{1,33},{33,65},{65,97},{98,2}... | collective-permute-start | bytes 423944 | tf_op jit(solution)/shard_map/ppermute | solution.py:20
  4.9 29.4 %collective-permute-start.2 = (bf16[96,16,128]{2,1,0:T(8,128)(2,1)S(1)}, bf16[96,16,128]{2,1,0:T(8,128)(2,1)}, u32[]{:S(2)}, u32[]{:S(2)}) collective-permute-start(bf16[96,16,128]{2,1,0:T(8,128)(2,1)S(1)} %slice.85), channel_id=1, source_target_pairs={{32,0},{64,32},{96,64},{0,96},{33,1},{65,33},{97,65},{1,97},{34,2}... | collective-permute-start | bytes 1179656 | tf_op jit(solution)/shard_map/ppermute | solution.py:20
  9.6 48.4 %collective-permute-start.1 = (bf16[416,16,128]{2,1,0:T(8,128)(2,1)}, bf16[416,16,128]{2,1,0:T(8,128)(2,1)}, u32[]{:S(2)}, u32[]{:S(2)}) collective-permute-start(bf16[416,16,128]{2,1,0:T(8,128)(2,1)} %slice.84), channel_id=1, source_target_pairs={{96,0},{0,32},{32,64},{64,96},{97,1},{1,33},{33,65},{65,97},{98,2}... | collective-permute-start | bytes 5111816 | tf_op jit(solution)/shard_map/ppermute | solution.py:20
  14.5 22.7 %all-to-all-start = ((f32[32,1,2178]{2,1,0:T(1,128)}), f32[32,1,2178]{2,1,0:T(1,128)S(1)}, u32[]{:S(2)}, u32[]{:S(2)}) async-start(f32[32,1,2178]{2,1,0:T(1,128)} %copy.35), calls=%async_computation | async-start | bytes 589824 | tf_op jit(solution)/shard_map/all_to_all | solution.py:202
  34.2 11.9 %collective-permute-start.3 = (bf16[96,16,128]{2,1,0:T(8,128)(2,1)}, bf16[96,16,128]{2,1,0:T(8,128)(2,1)}, u32[]{:S(2)}, u32[]{:S(2)}) collective-permute-start(bf16[96,16,128]{2,1,0:T(8,128)(2,1)} %collective-permute-done.2), channel_id=1, source_target_pairs={{32,0},{64,32},{96,64},{0,96},{33,1},{65,33},{97,65},{1,97},{34,2}... | collective-permute-start | bytes 1179656 | tf_op jit(solution)/shard_map/ppermute | solution.py:20
  39.0 10.9 %copy-start.5 = (f32[1024,64]{0,1:T(8,128)S(1)}, f32[1024,64]{0,1:T(8,128)}, u32[]{:S(2)}) copy-start(f32[1024,64]{0,1:T(8,128)} %copy.36) | copy-start | bytes 786436
  39.2 23.9 %copy-start.3 = (pred[1024,512]{1,0:T(32,128)(4,1)S(1)}, pred[1024,512]{1,0:T(32,128)(4,1)}, u32[]{:S(2)}) copy-start(pred[1024,512]{1,0:T(32,128)(4,1)} %iota_compare_fusion.4) | copy-start | bytes 1572868
  46.2 11.8 %collective-permute-start.4 = (bf16[96,16,128]{2,1,0:T(8,128)(2,1)}, bf16[96,16,128]{2,1,0:T(8,128)(2,1)S(1)}, u32[]{:S(2)}, u32[]{:S(2)}) collective-permute-start(bf16[96,16,128]{2,1,0:T(8,128)(2,1)} %collective-permute-done.3), channel_id=1, source_target_pairs={{32,0},{64,32},{96,64},{0,96},{33,1},{65,33},{97,65},{1,97},{34,2}... | collective-permute-start | bytes 1179656 | tf_op jit(solution)/shard_map/ppermute | solution.py:20
  59.5 10.5 %collective-permute-start.6 = (bf16[96,16,128]{2,1,0:T(8,128)(2,1)S(1)}, bf16[96,16,128]{2,1,0:T(8,128)(2,1)S(1)}, u32[]{:S(2)}, u32[]{:S(2)}) collective-permute-start(bf16[96,16,128]{2,1,0:T(8,128)(2,1)S(1)} %slice.87), channel_id=1, source_target_pairs={{32,0},{64,32},{96,64},{0,96},{33,1},{65,33},{97,65},{1,97},{34,2}... | collective-permute-start | bytes 1179656 | tf_op jit(solution)/shard_map/ppermute | solution.py:20
  63.1 46.1 %collective-permute-start.5 = (bf16[416,16,128]{2,1,0:T(8,128)(2,1)}, bf16[416,16,128]{2,1,0:T(8,128)(2,1)}, u32[]{:S(2)}, u32[]{:S(2)}) collective-permute-start(bf16[416,16,128]{2,1,0:T(8,128)(2,1)} %slice.86), channel_id=1, source_target_pairs={{96,0},{0,32},{32,64},{64,96},{97,1},{1,33},{33,65},{65,97},{98,2}... | collective-permute-start | bytes 5111816 | tf_op jit(solution)/shard_map/ppermute | solution.py:20
  70.0 14.6 %collective-permute-start.7 = (bf16[96,16,128]{2,1,0:T(8,128)(2,1)S(1)}, bf16[96,16,128]{2,1,0:T(8,128)(2,1)}, u32[]{:S(2)}, u32[]{:S(2)}) collective-permute-start(bf16[96,16,128]{2,1,0:T(8,128)(2,1)S(1)} %collective-permute-done.6), channel_id=1, source_target_pairs={{32,0},{64,32},{96,64},{0,96},{33,1},{65,33},{97,65},{1,97},{34,2}... | collective-permute-start | bytes 1179656 | tf_op jit(solution)/shard_map/ppermute | solution.py:20
  77.0 7.7 %copy-start.1 = (pred[512,1024]{1,0:T(8,128)(4,1)S(1)}, pred[512,1024]{1,0:T(8,128)(4,1)}, u32[]{:S(2)}) copy-start(pred[512,1024]{1,0:T(8,128)(4,1)} %get-tuple-element.38) | copy-start | bytes 1572868
  77.0 7.7 %copy-start.2 = (pred[512,1024]{1,0:T(8,128)(4,1)S(1)}, pred[512,1024]{1,0:T(8,128)(4,1)}, u32[]{:S(2)}) copy-start(pred[512,1024]{1,0:T(8,128)(4,1)} %get-tuple-element.39) | copy-start | bytes 1572868
  77.0 7.7 %copy-start.6 = (f32[16,1024]{1,0:T(8,128)S(1)}, f32[16,1024]{1,0:T(8,128)}, u32[]{:S(2)}) copy-start(f32[16,1024]{1,0:T(8,128)} %get-tuple-element.35) | copy-start | bytes 196612
  77.0 7.7 %copy-start.7 = (f32[16,1024]{1,0:T(8,128)S(1)}, f32[16,1024]{1,0:T(8,128)}, u32[]{:S(2)}) copy-start(f32[16,1024]{1,0:T(8,128)} %get-tuple-element.36) | copy-start | bytes 196612
  77.0 60.8 %all-to-all-start.3 = ((bf16[32,32,2048]{2,1,0:T(8,128)(2,1)}), bf16[32,32,2048]{2,1,0:T(8,128)(2,1)}, u32[]{:S(2)}, u32[]{:S(2)}) async-start(bf16[32,32,2048]{2,1,0:T(8,128)(2,1)} %bitcast.101), calls=%async_computation.3 | async-start | bytes 8388608 | tf_op jit(solution)/shard_map/all_to_all | solution.py:252
  84.6 24.6 %collective-permute-start.8 = (bf16[96,16,128]{2,1,0:T(8,128)(2,1)}, bf16[96,16,128]{2,1,0:T(8,128)(2,1)S(1)}, u32[]{:S(2)}, u32[]{:S(2)}) collective-permute-start(bf16[96,16,128]{2,1,0:T(8,128)(2,1)} %collective-permute-done.7), channel_id=1, source_target_pairs={{32,0},{64,32},{96,64},{0,96},{33,1},{65,33},{97,65},{1,97},{34,2}... | collective-permute-start | bytes 1179656 | tf_op jit(solution)/shard_map/ppermute | solution.py:20
  84.7 24.4 %copy-start.8 = (f32[512]{0:T(512)S(1)}, f32[512]{0:T(512)}, u32[]{:S(2)}) copy-start(f32[512]{0:T(512)} %param.13) | copy-start | bytes 6148
  84.7 24.4 %copy-start.4 = (pred[1024,512]{1,0:T(32,128)(4,1)S(1)}, pred[1024,512]{1,0:T(32,128)(4,1)}, u32[]{:S(2)}) copy-start(pred[1024,512]{1,0:T(32,128)(4,1)} %iota_compare_fusion.4) | copy-start | bytes 1572868
  137.7 59.2 %all-to-all-start.1 = ((bf16[32,32,2048]{2,1,0:T(8,128)(2,1)}), bf16[32,32,2048]{2,1,0:T(8,128)(2,1)}, u32[]{:S(2)}, u32[]{:S(2)}) async-start(bf16[32,32,2048]{2,1,0:T(8,128)(2,1)} %bitcast.102), calls=%async_computation.1 | async-start | bytes 8388608 | tf_op jit(solution)/shard_map/all_to_all | solution.py:252
  196.9 59.2 %all-to-all-start.4 = ((bf16[32,512,128]{2,1,0:T(8,128)(2,1)}), bf16[32,512,128]{2,1,0:T(8,128)(2,1)}, u32[]{:S(2)}, u32[]{:S(2)}) async-start(bf16[32,512,128]{2,1,0:T(8,128)(2,1)} %bitcast.105), calls=%async_computation.4 | async-start | bytes 8388608 | tf_op jit(solution)/shard_map/all_to_all | solution.py:260
  256.2 59.2 %all-to-all-start.2 = ((bf16[32,512,128]{2,1,0:T(8,128)(2,1)}), bf16[32,512,128]{2,1,0:T(8,128)(2,1)}, u32[]{:S(2)}, u32[]{:S(2)}) async-start(bf16[32,512,128]{2,1,0:T(8,128)(2,1)} %bitcast.106), calls=%async_computation.2 | async-start | bytes 8388608 | tf_op jit(solution)/shard_map/all_to_all | solution.py:260
  (1 other events, 2.8 us)

commit v4 on v2

--- a/solution.py
+++ b/solution.py
@@ -167,12 +167,21 @@
         axis=1,
     )
     moved_meta = shifted(meta, "body", 1)
-    moved_chunks = []
+    half = Q // 2
+    pieces = []
     for k in range(SPLIT):
         piece = master_basis[:, :, k * width:(k + 1) * width]
-        if moved_chunks:
-            piece, _ = lax.optimization_barrier((piece, moved_chunks[-1]))
-        moved_chunks.append(shifted(piece, "body", 1))
+        if k == 0:
+            for h in range(2):
+                part = piece[:, h * half:(h + 1) * half, :]
+                pieces.append(part.reshape(seg_count // 2, Q, width))
+        else:
+            pieces.append(piece)
+    moved_pieces = []
+    for piece in pieces:
+        if moved_pieces:
+            piece, _ = lax.optimization_barrier((piece, moved_pieces[-1]))
+        moved_pieces.append(shifted(piece, "body", 1))
 
     moved_dest = moved_meta[:, wcols].astype(i32)
     slot = slot_of(moved_dest, dom_count, capacity)
@@ -222,21 +231,21 @@
     ).reshape(tile_count, NP, Q * per_tile)
 
     staged = (tables, own, left, scale)
-    got_chunks = []
-    for k in range(SPLIT):
-        moved = moved_chunks[k]
-        if k == 1:
+    got_pieces = []
+    for j, moved in enumerate(moved_pieces):
+        if j == len(moved_pieces) - 1:
             moved, staged = lax.optimization_barrier((moved, staged))
             tables, own, left, scale = staged
             table_hi, table_lo, weight_sum = tables
+        cols = moved.size // seg_count
         packed = jnp.dot(
             placer.astype(bf16),
-            moved.reshape(seg_count, Q * width),
+            moved.reshape(seg_count, cols),
             preferred_element_type=f32,
         ).astype(bf16)
-        got_chunks.append(
-            lax.all_to_all(packed.reshape(dom_count, capacity, Q * width), "dom", 0, 0, tiled=True)
-        )
+        got = lax.all_to_all(packed.reshape(dom_count, capacity, cols), "dom", 0, 0, tiled=True)
+        got_pieces.append(got.reshape(slots, cols))
+    got_chunks = [jnp.concatenate(got_pieces[:2], axis=1), got_pieces[2]]
 
     coupling = None
     for k in range(SPLIT):

time: 311 us -> 322 us (1.035)
  starting transfers between devices: 39.6 us -> 47 us
  waiting for transfers between devices: 121 us -> 115 us
  other arithmetic: 29.8 us -> 33.9 us
  local copies, waits for them, and re-layouts: 28.2 us -> 32 us
    all_to_all x2 -> x3, starting transfers between devices: 15.7 us -> 23.1 us  [on_device(): lax.all_to_all(packed.reshape(dom_count, capacity, cols), 'dom', 0, 0, ti...]
    all_to_all x2 -> x3, waiting for transfers between devices: 9.24 us -> 5.09 us  [on_device(): lax.all_to_all(packed.reshape(dom_count, capacity, cols), 'dom', 0, 0, ti...]
    concatenate x0 -> x1, other arithmetic: none -> 4.15 us  [on_device(): got_chunks = [jnp.concatenate(got_pieces[:2], axis=1), got_pieces[2]]]
    dot_general x2 -> x3, matrix products: 10.3 us -> 12.3 us  [on_device(): jnp.dot(placer.astype(bf16), moved.reshape(seg_count, cols), preferred_el...]
    ppermute x3 -> x4, waiting for transfers between devices: 45 us -> 43.4 us  [shifted(): return lax.ppermute(block, axis, route)]
  transfers between devices with their start and end apart: 8 -> 10, of which waited for: 5 -> 7; matrix products, arithmetic and copies ran while one was open for 20% -> 24% of each run, Pallas kernels for 24% -> 23%
where the time goes in v4:
time: 322 us; the launch traced here: 321 us
  waiting for transfers between devices  115 us (36%)
  Pallas kernels  78.6 us (24%)
  starting transfers between devices  47 us (15%)
  other arithmetic  33.9 us (11%)
  local copies, waits for them, and re-layouts  32 us (10%)
  matrix products  14 us (4%)
    all_to_all x2, waiting for transfers between devices, on_device(): lax.all_to_all(packed_tiles.reshape(dom_count, tile_capacity * NP, width)...  66.5 us
    pallas_call x2, Pallas kernels, flux_chunk(): pl.pallas_call(flux_kernel, grid=(q_count,), in_specs=[pl.BlockSpec((1, s...  45.1 us
    ppermute x4, waiting for transfers between devices, shifted(): return lax.ppermute(block, axis, route)  43.4 us
    reduce_sum x1, other arithmetic, on_device(): weight_sum = jnp.sum(table, axis=2)  23.3 us
    pallas_call x2, Pallas kernels, packed_tiles_of(): pl.pallas_call(functools.partial(tile_kernel, tile_count, per_tile), in_s...  23.1 us
    all_to_all x3, starting transfers between devices, on_device(): lax.all_to_all(packed.reshape(dom_count, capacity, cols), 'dom', 0, 0, ti...  23.1 us
    dot_general x3, matrix products, on_device(): jnp.dot(placer.astype(bf16), moved.reshape(seg_count, cols), preferred_el...  12.3 us
    all_to_all x2, starting transfers between devices, on_device(): lax.all_to_all(packed_tiles.reshape(dom_count, tile_capacity * NP, width)...  12.1 us
  transfers between devices with their start and end apart: 10, of which 7 were waited for; matrix products, arithmetic and copies ran while one was open for 24% of the time, Pallas kernels for 23%

profile of v4, /device:TPU:32, one launch (start us, length us, event | category | flops | bytes accessed | tf_op | source)
XLA Modules:
  0.0 320.7 jit_solution(10120336237601904432)
XLA Ops:
  13.1 8.2 %all-to-all-start = ((f32[32,1,2178]{2,1,0:T(1,128)}), f32[32,1,2178]{2,1,0:T(1,128)S(1)}, u32[]{:S(2)}, u32[]{:S(2)}) async-start(f32[32,1,2178]{2,1,0:T(1,128)} %copy.35), calls=%async_computation | async-start | bytes 589824 | tf_op jit(solution)/shard_map/all_to_all | solution.py:204
  21.4 11.0 %collective-permute-done.1 = bf16[256,16,128]{2,1,0:T(8,128)(2,1)S(1)} collective-permute-done((bf16[256,16,128]{2,1,0:T(8,128)(2,1)S(1)}, bf16[256,16,128]{2,1,0:T(8,128)(2,1)S(1)}, u32[]{:S(2)}, u32[]{:S(2)}) %collective-permute-start.1) | collective-permute-done | bytes 1048608 | tf_op jit(solution)/shard_map/ppermute | solution.py:20
  35.5 8.2 %all-to-all-start.3 = ((bf16[32,32,1024]{2,1,0:T(8,128)(2,1)}), bf16[32,32,1024]{2,1,0:T(8,128)(2,1)S(1)}, u32[]{:S(2)}, u32[]{:S(2)}) async-start(bf16[32,32,1024]{2,1,0:T(8,128)(2,1)} %bitcast.102), calls=%async_computation.3 | async-start | bytes 4194304 | tf_op jit(solution)/shard_map/all_to_all | solution.py:246
  50.6 3.9 %copy.38 = bf16[32,256,16,16]{1,3,2,0:T(8,128)(2,1)} copy(bf16[32,256,16,16]{1,2,3,0:T(8,128)(2,1)S(1)} %bitcast.95) | data formatting | bytes 8388608 | tf_op jit(solution)/shard_map/transpose | solution.py:229
  61.9 20.5 %collective-permute-done.2 = bf16[256,16,128]{2,1,0:T(8,128)(2,1)} collective-permute-done((bf16[256,16,128]{2,1,0:T(8,128)(2,1)}, bf16[256,16,128]{2,1,0:T(8,128)(2,1)}, u32[]{:S(2)}, u32[]{:S(2)}) %collective-permute-start.2) | collective-permute-done | bytes 1048608 | tf_op jit(solution)/shard_map/ppermute | solution.py:20
  84.7 3.8 %fusion.8 = bf16[1024,1024]{1,0:T(8,128)(2,1)} fusion(bf16[512,1024]{1,0:T(8,128)(2,1)} %reshape.240, s32[512]{0:T(512)S(1)} %add.49), kind=kOutput, calls=%fused_computation.18 | convolution fusion | flops 1075314688 | bytes 3147776 | tf_op jit(solution)/shard_map/dot_general | solution.py:241
  88.4 7.4 %all-to-all-start.4 = ((bf16[32,32,1024]{2,1,0:T(8,128)(2,1)}), bf16[32,32,1024]{2,1,0:T(8,128)(2,1)}, u32[]{:S(2)}, u32[]{:S(2)}) async-start(bf16[32,32,1024]{2,1,0:T(8,128)(2,1)} %bitcast.103), calls=%async_computation.4 | async-start | bytes 4194304 | tf_op jit(solution)/shard_map/all_to_all | solution.py:246
  95.9 23.3 %fusion = (f32[16,512]{1,0:T(8,128)S(1)}, bf16[16,512,1024]{2,1,0:T(8,128)(2,1)}, bf16[16,512,1024]{2,1,0:T(8,128)(2,1)}) fusion(f32[16,1024]{1,0:T(8,128)} %get-tuple-element.37, f32[16,1024]{1,0:T(8,128)} %get-tuple-element.38, f32[16,1024]{1,0:T(8,128)} %get-tuple-element.39, f32[16,1024]{1,0:T(8,128)S(1)} %get-tuple-element.36, ...), kind=kLoop, calls=%fused_computation.2 | loop fusion | flops 100655104 | bytes 35946496 | tf_op jit(solution)/shard_map/reduce_sum | solution.py:220
  119.2 11.4 %collective-permute-done.3 = bf16[512,16,128]{2,1,0:T(8,128)(2,1)} collective-permute-done((bf16[512,16,128]{2,1,0:T(8,128)(2,1)}, bf16[512,16,128]{2,1,0:T(8,128)(2,1)}, u32[]{:S(2)}, u32[]{:S(2)}) %collective-permute-start.3) | collective-permute-done | bytes 2097184 | tf_op jit(solution)/shard_map/ppermute | solution.py:20
  130.7 5.9 %convolution_convert_fusion = bf16[1024,2048]{1,0:T(8,128)(2,1)} fusion(bf16[64,8,16,128]{3,2,1,0:T(8,128)(2,1)} %bitcast.46, s32[512]{0:T(512)S(1)} %add.49), kind=kOutput, calls=%fused_computation.6 | convolution fusion | flops 2150105088 | bytes 6293504 | tf_op jit(solution)/shard_map/dot_general | solution.py:241
  136.5 7.4 %all-to-all-start.1 = ((bf16[32,32,2048]{2,1,0:T(8,128)(2,1)}), bf16[32,32,2048]{2,1,0:T(8,128)(2,1)}, u32[]{:S(2)}, u32[]{:S(2)}) async-start(bf16[32,32,2048]{2,1,0:T(8,128)(2,1)} %bitcast.101), calls=%async_computation.1 | async-start | bytes 8388608 | tf_op jit(solution)/shard_map/all_to_all | solution.py:246
  144.6 4.1 %pad_maximum_fusion.rows_ref = bf16[1024,2048]{1,0:T(8,128)(2,1)} fusion(bf16[1024,1024]{1,0:T(8,128)(2,1)} %bitcast.34, bf16[1024,1024]{1,0:T(8,128)(2,1)S(1)} %bitcast.99), kind=kLoop, calls=%fused_computation.4 | loop fusion | flops 8388608 | bytes 8388608 | tf_op jit(solution)/shard_map/concatenate | solution.py:248
  148.8 6.4 %copy.40.left_ref = bf16[32,256,256]{2,1,0:T(8,128)(2,1)} copy(bf16[32,256,256]{1,2,0:T(8,128)(2,1)} %bitcast.96) | data formatting | bytes 8388608 | tf_op jit(solution)/shard_map/optimization_barrier | solution.py:237
  157.9 22.6 %shard_map.84.flux_ref = bf16[16,512,128]{2,1,0:T(8,128)(2,1)} custom-call(bf16[16,512,1024]{2,1,0:T(8,128)(2,1)} %get-tuple-element.22.hi_ref, bf16[16,512,1024]{2,1,0:T(8,128)(2,1)} %get-tuple-element.23.lo_ref, bf16[1024,2048]{1,0:T(8,128)(2,1)} %pad_maximum_fusion.rows_ref, bf16[16,512,256]{2,1,0:T(8,128)(2,1)} %bitcast.93, f32[16,512,1]{2,1,0:T(8,128)} %copy.39.scale_ref), custom_call_target="tpu_custom_call" | custom-call | tf_op jit(solution)/shard_map/pallas_call | solution.py:44
  180.4 11.6 %shard_map.85 = bf16[64,256,128]{2,1,0:T(8,128)(2,1)} custom-call(s32[64]{0:T(128)} %compare_select_fusion.source_ref, bf16[32,256,256]{2,1,0:T(8,128)(2,1)} %copy.40.left_ref, bf16[16,512,128]{2,1,0:T(8,128)(2,1)} %shard_map.84.flux_ref), custom_call_target="tpu_custom_call" | custom-call | tf_op jit(solution)/shard_map/pallas_call | solution.py:87
  192.1 5.1 %all-to-all-done.1 = bf16[32,32,2048]{2,1,0:T(8,128)(2,1)} async-done(((bf16[32,32,2048]{2,1,0:T(8,128)(2,1)}), bf16[32,32,2048]{2,1,0:T(8,128)(2,1)}, u32[]{:S(2)}, u32[]{:S(2)}) %all-to-all-start.1) | async-done | bytes 4194336 | tf_op jit(solution)/shard_map/all_to_all | solution.py:246
  197.2 6.0 %all-to-all-start.5 = ((bf16[32,512,128]{2,1,0:T(8,128)(2,1)}), bf16[32,512,128]{2,1,0:T(8,128)(2,1)}, u32[]{:S(2)}, u32[]{:S(2)}) async-start(bf16[32,512,128]{2,1,0:T(8,128)(2,1)} %bitcast.97), calls=%async_computation.5 | async-start | bytes 8388608 | tf_op jit(solution)/shard_map/all_to_all | solution.py:255
  203.2 22.5 %shard_map.82.flux_ref = bf16[16,512,128]{2,1,0:T(8,128)(2,1)} custom-call(bf16[16,512,1024]{2,1,0:T(8,128)(2,1)} %get-tuple-element.22.hi_ref, bf16[16,512,1024]{2,1,0:T(8,128)(2,1)} %get-tuple-element.23.lo_ref, bf16[1024,2048]{1,0:T(8,128)(2,1)} %bitcast.28.rows_ref, bf16[16,512,256]{2,1,0:T(8,128)(2,1)} %bitcast.94, f32[16,512,1]{2,1,0:T(8,128)} %copy.39.scale_ref), custom_call_target="tpu_custom_call" | custom-call | tf_op jit(solution)/shard_map/pallas_call | solution.py:44
  225.7 11.5 %shard_map.83 = bf16[64,256,128]{2,1,0:T(8,128)(2,1)} custom-call(s32[64]{0:T(128)} %compare_select_fusion.source_ref, bf16[32,256,256]{2,1,0:T(8,128)(2,1)} %copy.40.left_ref, bf16[16,512,128]{2,1,0:T(8,128)(2,1)} %shard_map.82.flux_ref), custom_call_target="tpu_custom_call" | custom-call | tf_op jit(solution)/shard_map/pallas_call | solution.py:87
  237.3 19.1 %all-to-all-done.5 = bf16[32,512,128]{2,1,0:T(8,128)(2,1)} async-done(((bf16[32,512,128]{2,1,0:T(8,128)(2,1)}), bf16[32,512,128]{2,1,0:T(8,128)(2,1)}, u32[]{:S(2)}, u32[]{:S(2)}) %all-to-all-start.5) | async-done | bytes 4194336 | tf_op jit(solution)/shard_map/all_to_all | solution.py:255
  256.4 6.0 %all-to-all-start.2 = ((bf16[32,512,128]{2,1,0:T(8,128)(2,1)}), bf16[32,512,128]{2,1,0:T(8,128)(2,1)}, u32[]{:S(2)}, u32[]{:S(2)}) async-start(bf16[32,512,128]{2,1,0:T(8,128)(2,1)} %bitcast.98), calls=%async_computation.2 | async-start | bytes 8388608 | tf_op jit(solution)/shard_map/all_to_all | solution.py:255
  263.0 5.2 %shard_map.86.refs_0_ = f32[16,256,256]{2,1,0:T(8,128)} custom-call(s32[64]{0:T(128)} %sub.24.rows_ref, bf16[64,256,128]{2,1,0:T(8,128)(2,1)} %bitcast.36.tiles_ref), custom_call_target="tpu_custom_call" | custom-call | tf_op jit(solution)/shard_map/pallas_call | solution.py:128
  268.2 47.4 %all-to-all-done.2 = bf16[32,512,128]{2,1,0:T(8,128)(2,1)} async-done(((bf16[32,512,128]{2,1,0:T(8,128)(2,1)}), bf16[32,512,128]{2,1,0:T(8,128)(2,1)}, u32[]{:S(2)}, u32[]{:S(2)}) %all-to-all-start.2) | async-done | bytes 4194336 | tf_op jit(solution)/shard_map/all_to_all | solution.py:255
  315.6 5.2 %shard_map.87 = f32[16,256,256]{2,1,0:T(8,128)} custom-call(s32[64]{0:T(128)} %sub.24.rows_ref, bf16[64,256,128]{2,1,0:T(8,128)(2,1)} %bitcast.30.tiles_ref, f32[16,256,256]{2,1,0:T(8,128)} %shard_map.86.refs_0_), custom_call_target="tpu_custom_call", output_to_operand_aliasing={{}: (2, {})} | custom-call | tf_op jit(solution)/shard_map/pallas_call | solution.py:128
  (61 shorter events, 36.6 us)
Async XLA Ops:
  0.0 8.0 %copy-start.2 = (s32[32,1]{0,1:T(1,128)S(1)}, s32[32,1]{0,1:T(1,128)}, u32[]{:S(2)}) copy-start(s32[32,1]{0,1:T(1,128)} %param.14) | copy-start | bytes 388
  0.0 8.3 %copy-start.3 = (s32[32]{0:T(128)S(1)}, s32[32]{0:T(128)}, u32[]{:S(2)}) copy-start(s32[32]{0:T(128)} %param.15) | copy-start | bytes 388
  2.3 6.9 %collective-permute-start = (f32[512,69]{0,1:T(8,128)S(1)}, f32[512,69]{0,1:T(8,128)S(1)}, u32[]{:S(2)}, u32[]{:S(2)}) collective-permute-start(f32[512,69]{0,1:T(8,128)S(1)} %pad_maximum_fusion.1), channel_id=1, source_target_pairs={{96,0},{0,32},{32,64},{64,96},{97,1},{1,33},{33,65},{65,97},{98,2}... | collective-permute-start | bytes 423944 | tf_op jit(solution)/shard_map/ppermute | solution.py:20
  6.5 25.8 %collective-permute-start.1 = (bf16[256,16,128]{2,1,0:T(8,128)(2,1)S(1)}, bf16[256,16,128]{2,1,0:T(8,128)(2,1)S(1)}, u32[]{:S(2)}, u32[]{:S(2)}) collective-permute-start(bf16[256,16,128]{2,1,0:T(8,128)(2,1)S(1)} %bitcast.108), channel_id=1, source_target_pairs={{96,0},{0,32},{32,64},{64,96},{97,1},{1,33},{33,65},{65,97},{98,2}... | collective-permute-start | bytes 3145736 | tf_op jit(solution)/shard_map/ppermute | solution.py:20
  13.1 22.3 %all-to-all-start = ((f32[32,1,2178]{2,1,0:T(1,128)}), f32[32,1,2178]{2,1,0:T(1,128)S(1)}, u32[]{:S(2)}, u32[]{:S(2)}) async-start(f32[32,1,2178]{2,1,0:T(1,128)} %copy.35), calls=%async_computation | async-start | bytes 589824 | tf_op jit(solution)/shard_map/all_to_all | solution.py:204
  35.5 53.0 %all-to-all-start.3 = ((bf16[32,32,1024]{2,1,0:T(8,128)(2,1)}), bf16[32,32,1024]{2,1,0:T(8,128)(2,1)S(1)}, u32[]{:S(2)}, u32[]{:S(2)}) async-start(bf16[32,32,1024]{2,1,0:T(8,128)(2,1)} %bitcast.102), calls=%async_computation.3 | async-start | bytes 4194304 | tf_op jit(solution)/shard_map/all_to_all | solution.py:246
  43.7 3.4 %copy-start = (bf16[512,16,256]{2,1,0:T(8,128)(2,1)S(1)}, bf16[512,16,256]{2,1,0:T(8,128)(2,1)}, u32[]{:S(2)}) copy-start(bf16[512,16,256]{2,1,0:T(8,128)(2,1)} %param.12) | copy-start | bytes 12582916
  55.4 27.0 %collective-permute-start.2 = (bf16[256,16,128]{2,1,0:T(8,128)(2,1)}, bf16[256,16,128]{2,1,0:T(8,128)(2,1)}, u32[]{:S(2)}, u32[]{:S(2)}) collective-permute-start(bf16[256,16,128]{2,1,0:T(8,128)(2,1)} %bitcast.107), channel_id=1, source_target_pairs={{96,0},{0,32},{32,64},{64,96},{97,1},{1,33},{33,65},{65,97},{98,2}... | collective-permute-start | bytes 3145736 | tf_op jit(solution)/shard_map/ppermute | solution.py:20
  82.3 48.3 %collective-permute-start.3 = (bf16[512,16,128]{2,1,0:T(8,128)(2,1)}, bf16[512,16,128]{2,1,0:T(8,128)(2,1)}, u32[]{:S(2)}, u32[]{:S(2)}) collective-permute-start(bf16[512,16,128]{2,1,0:T(8,128)(2,1)} %slice.69), channel_id=1, source_target_pairs={{96,0},{0,32},{32,64},{64,96},{97,1},{1,33},{33,65},{65,97},{98,2}... | collective-permute-start | bytes 6291464 | tf_op jit(solution)/shard_map/ppermute | solution.py:20
  88.4 48.1 %all-to-all-start.4 = ((bf16[32,32,1024]{2,1,0:T(8,128)(2,1)}), bf16[32,32,1024]{2,1,0:T(8,128)(2,1)}, u32[]{:S(2)}, u32[]{:S(2)}) async-start(bf16[32,32,1024]{2,1,0:T(8,128)(2,1)} %bitcast.103), calls=%async_computation.4 | async-start | bytes 4194304 | tf_op jit(solution)/shard_map/all_to_all | solution.py:246
  95.9 23.3 %copy-start.1 = (f32[512]{0:T(512)S(1)}, f32[512]{0:T(512)}, u32[]{:S(2)}) copy-start(f32[512]{0:T(512)} %param.13) | copy-start | bytes 6148
  136.5 60.6 %all-to-all-start.1 = ((bf16[32,32,2048]{2,1,0:T(8,128)(2,1)}), bf16[32,32,2048]{2,1,0:T(8,128)(2,1)}, u32[]{:S(2)}, u32[]{:S(2)}) async-start(bf16[32,32,2048]{2,1,0:T(8,128)(2,1)} %bitcast.101), calls=%async_computation.1 | async-start | bytes 8388608 | tf_op jit(solution)/shard_map/all_to_all | solution.py:246
  197.2 59.2 %all-to-all-start.5 = ((bf16[32,512,128]{2,1,0:T(8,128)(2,1)}), bf16[32,512,128]{2,1,0:T(8,128)(2,1)}, u32[]{:S(2)}, u32[]{:S(2)}) async-start(bf16[32,512,128]{2,1,0:T(8,128)(2,1)} %bitcast.97), calls=%async_computation.5 | async-start | bytes 8388608 | tf_op jit(solution)/shard_map/all_to_all | solution.py:255
  256.4 59.2 %all-to-all-start.2 = ((bf16[32,512,128]{2,1,0:T(8,128)(2,1)}), bf16[32,512,128]{2,1,0:T(8,128)(2,1)}, u32[]{:S(2)}, u32[]{:S(2)}) async-start(bf16[32,512,128]{2,1,0:T(8,128)(2,1)} %bitcast.98), calls=%async_computation.2 | async-start | bytes 8388608 | tf_op jit(solution)/shard_map/all_to_all | solution.py:255

commit v5 on v4

--- a/solution.py
+++ b/solution.py
@@ -177,10 +177,20 @@
                 pieces.append(part.reshape(seg_count // 2, Q, width))
         else:
             pieces.append(piece)
+    own = jnp.transpose(slave_basis, (1, 0, 2))
+    left = jnp.transpose(
+        slave_basis.reshape(tile_count, per_tile, Q, NP), (0, 3, 2, 1)
+    ).reshape(tile_count, NP, Q * per_tile)
     moved_pieces = []
-    for piece in pieces:
-        if moved_pieces:
-            piece, _ = lax.optimization_barrier((piece, moved_pieces[-1]))
+    for j in range(len(pieces)):
+        piece = pieces[j]
+        if j == 1:
+            piece, moved_pieces[-1], early = lax.optimization_barrier(
+                (piece, moved_pieces[-1], (own, left, pieces[2]))
+            )
+            own, left, pieces[2] = early
+        elif moved_pieces:
+            piece, moved_pieces[-1] = lax.optimization_barrier((piece, moved_pieces[-1]))
         moved_pieces.append(shifted(piece, "body", 1))
 
     moved_dest = moved_meta[:, wcols].astype(i32)
@@ -225,10 +235,6 @@
     got_rows = got_meta[:, capacity * rec_cols:].reshape(tile_slots).astype(i32) - 1
     tile_source = jnp.dot(tile_placer.astype(i32), jnp.arange(1, tile_count + 1, dtype=i32)) - 1
     tile_source = jnp.where(tile_source < 0, tile_count, tile_source)
-    own = jnp.transpose(slave_basis, (1, 0, 2))
-    left = jnp.transpose(
-        slave_basis.reshape(tile_count, per_tile, Q, NP), (0, 3, 2, 1)
-    ).reshape(tile_count, NP, Q * per_tile)
 
     staged = (tables, own, left, scale)
     got_pieces = []

time: 322 us -> 316 us (0.981)
  waiting for transfers between devices: 115 us -> 110 us
    ppermute x4, waiting for transfers between devices: 43.4 us -> 33.3 us  [shifted(): return lax.ppermute(block, axis, route)]
    all_to_all x1, waiting for transfers between devices: 0.01 us -> 4.36 us  [on_device(): got_meta = lax.all_to_all(send_meta, 'dom', 0, 0, tiled=True)]
  transfers between devices with their start and end apart: 10 -> 10, of which waited for: 7 -> 7; matrix products, arithmetic and copies ran while one was open for 24% -> 25% of each run, Pallas kernels for 23% -> 23%
where the time goes in v5:
time: 316 us; the launch traced here: 314 us
  waiting for transfers between devices  110 us (35%)
  Pallas kernels  77.8 us (25%)
  starting transfers between devices  45.5 us (14%)
  other arithmetic  34.2 us (11%)
  local copies, waits for them, and re-layouts  32.7 us (10%)
  matrix products  14 us (4%)
    all_to_all x2, waiting for transfers between devices, on_device(): lax.all_to_all(packed_tiles.reshape(dom_count, tile_capacity * NP, width)...  66.9 us
    pallas_call x2, Pallas kernels, flux_chunk(): pl.pallas_call(flux_kernel, grid=(q_count,), in_specs=[pl.BlockSpec((1, s...  45.1 us
    ppermute x4, waiting for transfers between devices, shifted(): return lax.ppermute(block, axis, route)  33.3 us
    reduce_sum x1, other arithmetic, on_device(): weight_sum = jnp.sum(table, axis=2)  23.3 us
    pallas_call x2, Pallas kernels, packed_tiles_of(): pl.pallas_call(functools.partial(tile_kernel, tile_count, per_tile), in_s...  23.1 us
    all_to_all x3, starting transfers between devices, on_device(): lax.all_to_all(packed.reshape(dom_count, capacity, cols), 'dom', 0, 0, ti...  20.7 us
    dot_general x3, matrix products, on_device(): jnp.dot(placer.astype(bf16), moved.reshape(seg_count, cols), preferred_el...  12.2 us
    all_to_all x2, starting transfers between devices, on_device(): lax.all_to_all(packed_tiles.reshape(dom_count, tile_capacity * NP, width)...  12.1 us
  transfers between devices with their start and end apart: 10, of which 7 were waited for; matrix products, arithmetic and copies ran while one was open for 25% of the time, Pallas kernels for 23%

profile of v5, /device:TPU:32, one launch (start us, length us, event | category | flops | bytes accessed | tf_op | source)
XLA Modules:
  0.0 314.0 jit_solution(12131486051825884797)
XLA Ops:
  10.6 5.9 %copy.54 = bf16[512,16,256]{2,0,1:T(8,128)(2,1)} copy(bf16[512,16,256]{2,1,0:T(8,128)(2,1)} %param.12) | data formatting | bytes 8388608 | tf_op args[4]
  16.5 3.9 %copy.37 = bf16[32,256,16,16]{1,3,2,0:T(8,128)(2,1)} copy(bf16[32,256,16,16]{1,2,3,0:T(8,128)(2,1)S(1)} %bitcast.95) | data formatting | bytes 8388608 | tf_op jit(solution)/shard_map/transpose | solution.py:181
  24.4 8.2 %all-to-all-start = ((f32[32,1,2178]{2,1,0:T(1,128)}), f32[32,1,2178]{2,1,0:T(1,128)S(1)}, u32[]{:S(2)}, u32[]{:S(2)}) async-start(f32[32,1,2178]{2,1,0:T(1,128)} %copy.35), calls=%async_computation | async-start | bytes 589824 | tf_op jit(solution)/shard_map/all_to_all | solution.py:214
  35.8 4.4 %all-to-all-done = f32[32,1,2178]{2,1,0:T(1,128)S(1)} async-done(((f32[32,1,2178]{2,1,0:T(1,128)}), f32[32,1,2178]{2,1,0:T(1,128)S(1)}, u32[]{:S(2)}, u32[]{:S(2)}) %all-to-all-start) | async-done | bytes 278816 | tf_op jit(solution)/shard_map/all_to_all | solution.py:214
  40.1 5.6 %all-to-all-start.3 = ((bf16[32,32,1024]{2,1,0:T(8,128)(2,1)}), bf16[32,32,1024]{2,1,0:T(8,128)(2,1)S(1)}, u32[]{:S(2)}, u32[]{:S(2)}) async-start(bf16[32,32,1024]{2,1,0:T(8,128)(2,1)} %bitcast.102), calls=%async_computation.3 | async-start | bytes 4194304 | tf_op jit(solution)/shard_map/all_to_all | solution.py:252
  54.0 19.6 %collective-permute-done.2 = bf16[256,16,128]{2,1,0:T(8,128)(2,1)} collective-permute-done((bf16[256,16,128]{2,1,0:T(8,128)(2,1)}, bf16[256,16,128]{2,1,0:T(8,128)(2,1)}, u32[]{:S(2)}, u32[]{:S(2)}) %collective-permute-start.2) | collective-permute-done | bytes 1048608 | tf_op jit(solution)/shard_map/ppermute | solution.py:20
  79.6 7.5 %all-to-all-start.4 = ((bf16[32,32,1024]{2,1,0:T(8,128)(2,1)}), bf16[32,32,1024]{2,1,0:T(8,128)(2,1)}, u32[]{:S(2)}, u32[]{:S(2)}) async-start(bf16[32,32,1024]{2,1,0:T(8,128)(2,1)} %bitcast.103), calls=%async_computation.4 | async-start | bytes 4194304 | tf_op jit(solution)/shard_map/all_to_all | solution.py:252
  87.2 23.3 %fusion = (f32[16,512]{1,0:T(8,128)S(1)}, bf16[16,512,1024]{2,1,0:T(8,128)(2,1)}, bf16[16,512,1024]{2,1,0:T(8,128)(2,1)}) fusion(f32[16,1024]{1,0:T(8,128)} %get-tuple-element.47, f32[16,1024]{1,0:T(8,128)} %get-tuple-element.48, f32[16,1024]{1,0:T(8,128)} %get-tuple-element.49, f32[16,1024]{1,0:T(8,128)S(1)} %get-tuple-element.46, ...), kind=kLoop, calls=%fused_computation.2 | loop fusion | flops 100655104 | bytes 35946496 | tf_op jit(solution)/shard_map/reduce_sum | solution.py:230
  110.5 13.6 %collective-permute-done.3 = bf16[512,16,128]{2,1,0:T(8,128)(2,1)} collective-permute-done((bf16[512,16,128]{2,1,0:T(8,128)(2,1)}, bf16[512,16,128]{2,1,0:T(8,128)(2,1)}, u32[]{:S(2)}, u32[]{:S(2)}) %collective-permute-start.3) | collective-permute-done | bytes 2097184 | tf_op jit(solution)/shard_map/ppermute | solution.py:20
  124.2 5.9 %convolution_convert_fusion = bf16[1024,2048]{1,0:T(8,128)(2,1)} fusion(bf16[64,8,16,128]{3,2,1,0:T(8,128)(2,1)} %bitcast.46, s32[512]{0:T(512)S(1)} %add.49), kind=kOutput, calls=%fused_computation.6 | convolution fusion | flops 2150105088 | bytes 6293504 | tf_op jit(solution)/shard_map/dot_general | solution.py:247
  130.1 7.5 %all-to-all-start.1 = ((bf16[32,32,2048]{2,1,0:T(8,128)(2,1)}), bf16[32,32,2048]{2,1,0:T(8,128)(2,1)}, u32[]{:S(2)}, u32[]{:S(2)}) async-start(bf16[32,32,2048]{2,1,0:T(8,128)(2,1)} %bitcast.101), calls=%async_computation.1 | async-start | bytes 8388608 | tf_op jit(solution)/shard_map/all_to_all | solution.py:252
  138.2 4.1 %pad_maximum_fusion.rows_ref = bf16[1024,2048]{1,0:T(8,128)(2,1)} fusion(bf16[1024,1024]{1,0:T(8,128)(2,1)} %bitcast.34, bf16[1024,1024]{1,0:T(8,128)(2,1)S(1)} %bitcast.99), kind=kLoop, calls=%fused_computation.4 | loop fusion | flops 8388608 | bytes 8388608 | tf_op jit(solution)/shard_map/concatenate | solution.py:254
  142.4 6.4 %copy.40.left_ref = bf16[32,256,256]{2,1,0:T(8,128)(2,1)} copy(bf16[32,256,256]{1,2,0:T(8,128)(2,1)} %bitcast.96) | data formatting | bytes 8388608 | tf_op jit(solution)/shard_map/optimization_barrier | solution.py:243
  151.5 22.6 %shard_map.84.flux_ref = bf16[16,512,128]{2,1,0:T(8,128)(2,1)} custom-call(bf16[16,512,1024]{2,1,0:T(8,128)(2,1)} %get-tuple-element.30.hi_ref, bf16[16,512,1024]{2,1,0:T(8,128)(2,1)} %get-tuple-element.31.lo_ref, bf16[1024,2048]{1,0:T(8,128)(2,1)} %pad_maximum_fusion.rows_ref, bf16[16,512,256]{2,1,0:T(8,128)(2,1)} %bitcast.93, f32[16,512,1]{2,1,0:T(8,128)} %copy.39.scale_ref), custom_call_target="tpu_custom_call" | custom-call | tf_op jit(solution)/shard_map/pallas_call | solution.py:44
  174.1 11.6 %shard_map.85 = bf16[64,256,128]{2,1,0:T(8,128)(2,1)} custom-call(s32[64]{0:T(128)} %compare_select_fusion.source_ref, bf16[32,256,256]{2,1,0:T(8,128)(2,1)} %copy.40.left_ref, bf16[16,512,128]{2,1,0:T(8,128)(2,1)} %shard_map.84.flux_ref), custom_call_target="tpu_custom_call" | custom-call | tf_op jit(solution)/shard_map/pallas_call | solution.py:87
  185.7 5.1 %all-to-all-done.1 = bf16[32,32,2048]{2,1,0:T(8,128)(2,1)} async-done(((bf16[32,32,2048]{2,1,0:T(8,128)(2,1)}), bf16[32,32,2048]{2,1,0:T(8,128)(2,1)}, u32[]{:S(2)}, u32[]{:S(2)}) %all-to-all-start.1) | async-done | bytes 4194336 | tf_op jit(solution)/shard_map/all_to_all | solution.py:252
  190.8 6.0 %all-to-all-start.5 = ((bf16[32,512,128]{2,1,0:T(8,128)(2,1)}), bf16[32,512,128]{2,1,0:T(8,128)(2,1)}, u32[]{:S(2)}, u32[]{:S(2)}) async-start(bf16[32,512,128]{2,1,0:T(8,128)(2,1)} %bitcast.97), calls=%async_computation.5 | async-start | bytes 8388608 | tf_op jit(solution)/shard_map/all_to_all | solution.py:261
  196.8 22.5 %shard_map.82.flux_ref = bf16[16,512,128]{2,1,0:T(8,128)(2,1)} custom-call(bf16[16,512,1024]{2,1,0:T(8,128)(2,1)} %get-tuple-element.30.hi_ref, bf16[16,512,1024]{2,1,0:T(8,128)(2,1)} %get-tuple-element.31.lo_ref, bf16[1024,2048]{1,0:T(8,128)(2,1)} %bitcast.28.rows_ref, bf16[16,512,256]{2,1,0:T(8,128)(2,1)} %bitcast.94, f32[16,512,1]{2,1,0:T(8,128)} %copy.39.scale_ref), custom_call_target="tpu_custom_call" | custom-call | tf_op jit(solution)/shard_map/pallas_call | solution.py:44
  219.4 11.5 %shard_map.83 = bf16[64,256,128]{2,1,0:T(8,128)(2,1)} custom-call(s32[64]{0:T(128)} %compare_select_fusion.source_ref, bf16[32,256,256]{2,1,0:T(8,128)(2,1)} %copy.40.left_ref, bf16[16,512,128]{2,1,0:T(8,128)(2,1)} %shard_map.82.flux_ref), custom_call_target="tpu_custom_call" | custom-call | tf_op jit(solution)/shard_map/pallas_call | solution.py:87
  230.9 19.1 %all-to-all-done.5 = bf16[32,512,128]{2,1,0:T(8,128)(2,1)} async-done(((bf16[32,512,128]{2,1,0:T(8,128)(2,1)}), bf16[32,512,128]{2,1,0:T(8,128)(2,1)}, u32[]{:S(2)}, u32[]{:S(2)}) %all-to-all-start.5) | async-done | bytes 4194336 | tf_op jit(solution)/shard_map/all_to_all | solution.py:261
  250.0 6.0 %all-to-all-start.2 = ((bf16[32,512,128]{2,1,0:T(8,128)(2,1)}), bf16[32,512,128]{2,1,0:T(8,128)(2,1)}, u32[]{:S(2)}, u32[]{:S(2)}) async-start(bf16[32,512,128]{2,1,0:T(8,128)(2,1)} %bitcast.98), calls=%async_computation.2 | async-start | bytes 8388608 | tf_op jit(solution)/shard_map/all_to_all | solution.py:261
  256.6 4.8 %shard_map.86.refs_0_ = f32[16,256,256]{2,1,0:T(8,128)} custom-call(s32[64]{0:T(128)} %sub.24.rows_ref, bf16[64,256,128]{2,1,0:T(8,128)(2,1)} %bitcast.36.tiles_ref), custom_call_target="tpu_custom_call" | custom-call | tf_op jit(solution)/shard_map/pallas_call | solution.py:128
  261.4 47.8 %all-to-all-done.2 = bf16[32,512,128]{2,1,0:T(8,128)(2,1)} async-done(((bf16[32,512,128]{2,1,0:T(8,128)(2,1)}), bf16[32,512,128]{2,1,0:T(8,128)(2,1)}, u32[]{:S(2)}, u32[]{:S(2)}) %all-to-all-start.2) | async-done | bytes 4194336 | tf_op jit(solution)/shard_map/all_to_all | solution.py:261
  309.2 4.8 %shard_map.87 = f32[16,256,256]{2,1,0:T(8,128)} custom-call(s32[64]{0:T(128)} %sub.24.rows_ref, bf16[64,256,128]{2,1,0:T(8,128)(2,1)} %bitcast.30.tiles_ref, f32[16,256,256]{2,1,0:T(8,128)} %shard_map.86.refs_0_), custom_call_target="tpu_custom_call", output_to_operand_aliasing={{}: (2, {})} | custom-call | tf_op jit(solution)/shard_map/pallas_call | solution.py:128
  (63 shorter events, 35.9 us)
Async XLA Ops:
  0.0 8.3 %copy-start.1 = (bf16[512,16,256]{2,1,0:T(8,128)(2,1)S(1)}, bf16[512,16,256]{2,1,0:T(8,128)(2,1)}, u32[]{:S(2)}) copy-start(bf16[512,16,256]{2,1,0:T(8,128)(2,1)} %param.8) | copy-start | bytes 12582916
  2.6 7.4 %copy-start.3 = (s32[32,1]{0,1:T(1,128)S(1)}, s32[32,1]{0,1:T(1,128)}, u32[]{:S(2)}) copy-start(s32[32,1]{0,1:T(1,128)} %param.14) | copy-start | bytes 388
  2.6 7.7 %copy-start.4 = (s32[32]{0:T(128)S(1)}, s32[32]{0:T(128)}, u32[]{:S(2)}) copy-start(s32[32]{0:T(128)} %param.15) | copy-start | bytes 388
  2.6 17.8 %collective-permute-start = (f32[512,69]{0,1:T(8,128)S(1)}, f32[512,69]{0,1:T(8,128)S(1)}, u32[]{:S(2)}, u32[]{:S(2)}) collective-permute-start(f32[512,69]{0,1:T(8,128)S(1)} %pad_maximum_fusion.1), channel_id=1, source_target_pairs={{96,0},{0,32},{32,64},{64,96},{97,1},{1,33},{33,65},{65,97},{98,2}... | collective-permute-start | bytes 423944 | tf_op jit(solution)/shard_map/ppermute | solution.py:20
  6.8 25.8 %collective-permute-start.1 = (bf16[256,16,128]{2,1,0:T(8,128)(2,1)S(1)}, bf16[256,16,128]{2,1,0:T(8,128)(2,1)S(1)}, u32[]{:S(2)}, u32[]{:S(2)}) collective-permute-start(bf16[256,16,128]{2,1,0:T(8,128)(2,1)S(1)} %bitcast.108), channel_id=1, source_target_pairs={{96,0},{0,32},{32,64},{64,96},{97,1},{1,33},{33,65},{65,97},{98,2}... | collective-permute-start | bytes 3145736 | tf_op jit(solution)/shard_map/ppermute | solution.py:20
  10.6 5.9 %copy-start = (bf16[512,16,256]{2,1,0:T(8,128)(2,1)S(1)}, bf16[512,16,256]{2,1,0:T(8,128)(2,1)}, u32[]{:S(2)}) copy-start(bf16[512,16,256]{2,1,0:T(8,128)(2,1)} %param.12) | copy-start | bytes 12582916
  24.4 15.8 %all-to-all-start = ((f32[32,1,2178]{2,1,0:T(1,128)}), f32[32,1,2178]{2,1,0:T(1,128)S(1)}, u32[]{:S(2)}, u32[]{:S(2)}) async-start(f32[32,1,2178]{2,1,0:T(1,128)} %copy.35), calls=%async_computation | async-start | bytes 589824 | tf_op jit(solution)/shard_map/all_to_all | solution.py:214
  40.1 39.5 %all-to-all-start.3 = ((bf16[32,32,1024]{2,1,0:T(8,128)(2,1)}), bf16[32,32,1024]{2,1,0:T(8,128)(2,1)S(1)}, u32[]{:S(2)}, u32[]{:S(2)}) async-start(bf16[32,32,1024]{2,1,0:T(8,128)(2,1)} %bitcast.102), calls=%async_computation.3 | async-start | bytes 4194304 | tf_op jit(solution)/shard_map/all_to_all | solution.py:252
  46.6 27.0 %collective-permute-start.2 = (bf16[256,16,128]{2,1,0:T(8,128)(2,1)}, bf16[256,16,128]{2,1,0:T(8,128)(2,1)}, u32[]{:S(2)}, u32[]{:S(2)}) collective-permute-start(bf16[256,16,128]{2,1,0:T(8,128)(2,1)} %bitcast.107), channel_id=1, source_target_pairs={{96,0},{0,32},{32,64},{64,96},{97,1},{1,33},{33,65},{65,97},{98,2}... | collective-permute-start | bytes 3145736 | tf_op jit(solution)/shard_map/ppermute | solution.py:20
  75.8 48.3 %collective-permute-start.3 = (bf16[512,16,128]{2,1,0:T(8,128)(2,1)}, bf16[512,16,128]{2,1,0:T(8,128)(2,1)}, u32[]{:S(2)}, u32[]{:S(2)}) collective-permute-start(bf16[512,16,128]{2,1,0:T(8,128)(2,1)} %slice.71), channel_id=1, source_target_pairs={{96,0},{0,32},{32,64},{64,96},{97,1},{1,33},{33,65},{65,97},{98,2}... | collective-permute-start | bytes 6291464 | tf_op jit(solution)/shard_map/ppermute | solution.py:20
  79.6 50.4 %all-to-all-start.4 = ((bf16[32,32,1024]{2,1,0:T(8,128)(2,1)}), bf16[32,32,1024]{2,1,0:T(8,128)(2,1)}, u32[]{:S(2)}, u32[]{:S(2)}) async-start(bf16[32,32,1024]{2,1,0:T(8,128)(2,1)} %bitcast.103), calls=%async_computation.4 | async-start | bytes 4194304 | tf_op jit(solution)/shard_map/all_to_all | solution.py:252
  87.2 23.3 %copy-start.2 = (f32[512]{0:T(512)S(1)}, f32[512]{0:T(512)}, u32[]{:S(2)}) copy-start(f32[512]{0:T(512)} %param.13) | copy-start | bytes 6148
  130.1 60.7 %all-to-all-start.1 = ((bf16[32,32,2048]{2,1,0:T(8,128)(2,1)}), bf16[32,32,2048]{2,1,0:T(8,128)(2,1)}, u32[]{:S(2)}, u32[]{:S(2)}) async-start(bf16[32,32,2048]{2,1,0:T(8,128)(2,1)} %bitcast.101), calls=%async_computation.1 | async-start | bytes 8388608 | tf_op jit(solution)/shard_map/all_to_all | solution.py:252
  190.8 59.2 %all-to-all-start.5 = ((bf16[32,512,128]{2,1,0:T(8,128)(2,1)}), bf16[32,512,128]{2,1,0:T(8,128)(2,1)}, u32[]{:S(2)}, u32[]{:S(2)}) async-start(bf16[32,512,128]{2,1,0:T(8,128)(2,1)} %bitcast.97), calls=%async_computation.5 | async-start | bytes 8388608 | tf_op jit(solution)/shard_map/all_to_all | solution.py:261
  250.0 59.2 %all-to-all-start.2 = ((bf16[32,512,128]{2,1,0:T(8,128)(2,1)}), bf16[32,512,128]{2,1,0:T(8,128)(2,1)}, u32[]{:S(2)}, u32[]{:S(2)}) async-start(bf16[32,512,128]{2,1,0:T(8,128)(2,1)} %bitcast.98), calls=%async_computation.2 | async-start | bytes 8388608 | tf_op jit(solution)/shard_map/all_to_all | solution.py:261

commit v6 on v2

--- a/solution.py
+++ b/solution.py
@@ -114,10 +114,12 @@
 
 def assemble(rows, tiles, previous, chunk):
     tile_slots, depth, width = tiles.shape
-    blocks = BR, depth, width
+    steps = 4
+    band = depth // steps
+    blocks = BR, band, width
     specs = [
         pl.BlockSpec(memory_space=pltpu.SMEM),
-        pl.BlockSpec(tiles.shape, lambda i: (0, 0, 0)),
+        pl.BlockSpec((tile_slots, band, width), lambda i: (0, i, 0)),
     ]
     operands = [rows, tiles]
     aliases = {}
@@ -127,9 +129,9 @@
         aliases = {2: 0}
     return pl.pallas_call(
         assemble_kernel,
-        grid=(1,),
+        grid=(steps,),
         in_specs=specs,
-        out_specs=pl.BlockSpec(blocks, lambda i: (0, 0, chunk)),
+        out_specs=pl.BlockSpec(blocks, lambda i: (0, i, chunk)),
         out_shape=jax.ShapeDtypeStruct((BR, depth, width * SPLIT), jnp.float32),
         input_output_aliases=aliases,
     )(*operands)
@@ -177,6 +179,7 @@
     moved_dest = moved_meta[:, wcols].astype(i32)
     slot = slot_of(moved_dest, dom_count, capacity)
     placer = placer_of(slot, slots)
+    select = lax.optimization_barrier(placer.astype(bf16))
     records = jnp.concatenate([moved_meta[:, :wcols], moved_meta[:, wcols + 1:]], axis=1)
     packed_meta = jnp.dot(placer.astype(f32), records, precision=lax.Precision.HIGHEST)
     rec_cols = records.shape[1]
@@ -230,7 +233,7 @@
             tables, own, left, scale = staged
             table_hi, table_lo, weight_sum = tables
         packed = jnp.dot(
-            placer.astype(bf16),
+            select,
             moved.reshape(seg_count, Q * width),
             preferred_element_type=f32,
         ).astype(bf16)

time: 311 us -> 314 us (level)
  Pallas kernels: 77.8 us -> 81.4 us
    pallas_call x2, Pallas kernels: 9.61 us -> 13.2 us  [assemble(): pl.pallas_call(assemble_kernel, grid=(steps,), in_specs=specs, out_specs=...]
where the time goes in v6:
time: 314 us; the launch traced here: 312 us
  waiting for transfers between devices  120 us (38%)
  Pallas kernels  81.4 us (26%)
  starting transfers between devices  39.6 us (13%)
  other arithmetic  30 us (10%)
  local copies, waits for them, and re-layouts  28.2 us (9%)
  matrix products  12.1 us (4%)
    all_to_all x2, waiting for transfers between devices, on_device(): lax.all_to_all(packed_tiles.reshape(dom_count, tile_capacity * NP, width)...  65 us
    ppermute x3, waiting for transfers between devices, shifted(): return lax.ppermute(block, axis, route)  45.9 us
    pallas_call x2, Pallas kernels, flux_chunk(): pl.pallas_call(flux_kernel, grid=(q_count,), in_specs=[pl.BlockSpec((1, s...  45.1 us
    reduce_sum x1, other arithmetic, on_device(): weight_sum = jnp.sum(table, axis=2)  24.2 us
    pallas_call x2, Pallas kernels, packed_tiles_of(): pl.pallas_call(functools.partial(tile_kernel, tile_count, per_tile), in_s...  23.2 us
    all_to_all x2, starting transfers between devices, on_device(): lax.all_to_all(packed.reshape(dom_count, capacity, Q * width), 'dom', 0,...  15.7 us
    pallas_call x2, Pallas kernels, assemble(): pl.pallas_call(assemble_kernel, grid=(steps,), in_specs=specs, out_specs=...  13.2 us
    all_to_all x2, starting transfers between devices, on_device(): lax.all_to_all(packed_tiles.reshape(dom_count, tile_capacity * NP, width)...  12.1 us
  transfers between devices with their start and end apart: 8, of which 5 were waited for; matrix products, arithmetic and copies ran while one was open for 20% of the time, Pallas kernels for 24%

profile of v6, /device:TPU:32, one launch (start us, length us, event | category | flops | bytes accessed | tf_op | source)
XLA Modules:
  0.0 311.8 jit_solution(15746677788781244063)
XLA Ops:
  3.8 4.9 %fusion.29 = (bf16[512,16,128]{2,1,0:T(8,128)(2,1)}, bf16[512,16,128]{2,1,0:T(8,128)(2,1)}) fusion(bf16[512,16,256]{2,1,0:T(8,128)(2,1)} %param.8), kind=kLoop, calls=%fused_computation.71 | loop fusion | bytes 8388608 | tf_op jit(solution)/shard_map/slice | solution.py:174
  14.9 8.2 %all-to-all-start = ((f32[32,1,2178]{2,1,0:T(1,128)}), f32[32,1,2178]{2,1,0:T(1,128)S(1)}, u32[]{:S(2)}, u32[]{:S(2)}) async-start(f32[32,1,2178]{2,1,0:T(1,128)} %copy.35), calls=%async_computation | async-start | bytes 589824 | tf_op jit(solution)/shard_map/all_to_all | solution.py:198
  23.1 5.9 %copy.59 = bf16[512,16,256]{2,0,1:T(8,128)(2,1)} copy(bf16[512,16,256]{2,1,0:T(8,128)(2,1)} %param.12) | data formatting | bytes 8388608 | tf_op args[4]
  29.0 3.9 %copy.38 = bf16[32,256,16,16]{1,3,2,0:T(8,128)(2,1)} copy(bf16[32,256,16,16]{1,2,3,0:T(8,128)(2,1)S(1)} %bitcast.95) | data formatting | bytes 8388608 | tf_op jit(solution)/shard_map/transpose | solution.py:223
  36.1 21.3 %collective-permute-done.1 = bf16[512,16,128]{2,1,0:T(8,128)(2,1)} collective-permute-done((bf16[512,16,128]{2,1,0:T(8,128)(2,1)}, bf16[512,16,128]{2,1,0:T(8,128)(2,1)}, u32[]{:S(2)}, u32[]{:S(2)}) %collective-permute-start.1) | collective-permute-done | bytes 2097184 | tf_op jit(solution)/shard_map/ppermute | solution.py:20
  57.4 6.0 %convolution_convert_fusion = bf16[1024,2048]{1,0:T(8,128)(2,1)} fusion(bf16[1024,512]{1,0:T(8,128)(2,1)S(1)} %fusion.6, bf16[64,8,16,128]{3,2,1,0:T(8,128)(2,1)} %bitcast.44), kind=kOutput, calls=%fused_computation.5 | convolution fusion | flops 2149580800 | bytes 7340032 | tf_op jit(solution)/shard_map/dot_general | solution.py:235
  63.3 8.3 %all-to-all-start.3 = ((bf16[32,32,2048]{2,1,0:T(8,128)(2,1)}), bf16[32,32,2048]{2,1,0:T(8,128)(2,1)}, u32[]{:S(2)}, u32[]{:S(2)}) async-start(bf16[32,32,2048]{2,1,0:T(8,128)(2,1)} %bitcast.100), calls=%async_computation.3 | async-start | bytes 8388608 | tf_op jit(solution)/shard_map/all_to_all | solution.py:241
  73.0 24.2 %fusion = (f32[16,512]{1,0:T(8,128)S(1)}, bf16[16,512,1024]{2,1,0:T(8,128)(2,1)}, bf16[16,512,1024]{2,1,0:T(8,128)(2,1)}) fusion(f32[16,1024]{1,0:T(8,128)S(1)} %get-tuple-element.35, f32[16,1024]{1,0:T(8,128)S(1)} %get-tuple-element.36, f32[16,1024]{1,0:T(8,128)S(1)} %get-tuple-element.37, f32[16,1024]{1,0:T(8,128)S(1)} %get-tuple-element.34, ...), kind=kLoop, calls=%fused_computation.2 | loop fusion | flops 100655104 | bytes 35946496 | tf_op jit(solution)/shard_map/reduce_sum | solution.py:214
  97.2 24.6 %collective-permute-done.2 = bf16[512,16,128]{2,1,0:T(8,128)(2,1)S(1)} collective-permute-done((bf16[512,16,128]{2,1,0:T(8,128)(2,1)}, bf16[512,16,128]{2,1,0:T(8,128)(2,1)S(1)}, u32[]{:S(2)}, u32[]{:S(2)}) %collective-permute-start.2) | collective-permute-done | bytes 2097184 | tf_op jit(solution)/shard_map/ppermute | solution.py:20
  121.8 4.3 %convolution_convert_fusion.1 = bf16[1024,2048]{1,0:T(8,128)(2,1)} fusion(bf16[1024,512]{1,0:T(8,128)(2,1)S(1)} %copy-done.2, bf16[64,8,16,128]{3,2,1,0:T(8,128)(2,1)S(1)} %bitcast.110), kind=kOutput, calls=%fused_computation.6 | convolution fusion | flops 2149580800 | bytes 7340032 | tf_op jit(solution)/shard_map/dot_general | solution.py:235
  126.1 7.4 %all-to-all-start.1 = ((bf16[32,32,2048]{2,1,0:T(8,128)(2,1)}), bf16[32,32,2048]{2,1,0:T(8,128)(2,1)}, u32[]{:S(2)}, u32[]{:S(2)}) async-start(bf16[32,32,2048]{2,1,0:T(8,128)(2,1)} %bitcast.101), calls=%async_computation.1 | async-start | bytes 8388608 | tf_op jit(solution)/shard_map/all_to_all | solution.py:241
  134.3 6.4 %copy.40.left_ref = bf16[32,256,256]{2,1,0:T(8,128)(2,1)} copy(bf16[32,256,256]{1,2,0:T(8,128)(2,1)} %bitcast.96) | data formatting | bytes 8388608 | tf_op jit(solution)/shard_map/optimization_barrier | solution.py:232
  140.7 2.7 copy.39.scale_ref
  143.3 22.5 %shard_map.84.flux_ref = bf16[16,512,128]{2,1,0:T(8,128)(2,1)} custom-call(bf16[16,512,1024]{2,1,0:T(8,128)(2,1)} %get-tuple-element.20.hi_ref, bf16[16,512,1024]{2,1,0:T(8,128)(2,1)} %get-tuple-element.21.lo_ref, bf16[1024,2048]{1,0:T(8,128)(2,1)} %bitcast.30.rows_ref, bf16[16,512,256]{2,1,0:T(8,128)(2,1)} %bitcast.93, f32[16,512,1]{2,1,0:T(8,128)} %copy.39.scale_ref), custom_call_target="tpu_custom_call" | custom-call | tf_op jit(solution)/shard_map/pallas_call | solution.py:44
  165.9 11.6 %shard_map.85 = bf16[64,256,128]{2,1,0:T(8,128)(2,1)} custom-call(s32[64]{0:T(128)} %compare_select_fusion.source_ref, bf16[32,256,256]{2,1,0:T(8,128)(2,1)} %copy.40.left_ref, bf16[16,512,128]{2,1,0:T(8,128)(2,1)} %shard_map.84.flux_ref), custom_call_target="tpu_custom_call" | custom-call | tf_op jit(solution)/shard_map/pallas_call | solution.py:87
  177.5 9.2 %all-to-all-done.1 = bf16[32,32,2048]{2,1,0:T(8,128)(2,1)} async-done(((bf16[32,32,2048]{2,1,0:T(8,128)(2,1)}), bf16[32,32,2048]{2,1,0:T(8,128)(2,1)}, u32[]{:S(2)}, u32[]{:S(2)}) %all-to-all-start.1) | async-done | bytes 4194336 | tf_op jit(solution)/shard_map/all_to_all | solution.py:241
  186.7 6.0 %all-to-all-start.4 = ((bf16[32,512,128]{2,1,0:T(8,128)(2,1)}), bf16[32,512,128]{2,1,0:T(8,128)(2,1)}, u32[]{:S(2)}, u32[]{:S(2)}) async-start(bf16[32,512,128]{2,1,0:T(8,128)(2,1)} %bitcast.97), calls=%async_computation.4 | async-start | bytes 8388608 | tf_op jit(solution)/shard_map/all_to_all | solution.py:249
  192.8 22.6 %shard_map.82.flux_ref = bf16[16,512,128]{2,1,0:T(8,128)(2,1)} custom-call(bf16[16,512,1024]{2,1,0:T(8,128)(2,1)} %get-tuple-element.20.hi_ref, bf16[16,512,1024]{2,1,0:T(8,128)(2,1)} %get-tuple-element.21.lo_ref, bf16[1024,2048]{1,0:T(8,128)(2,1)} %bitcast.26.rows_ref, bf16[16,512,256]{2,1,0:T(8,128)(2,1)} %bitcast.94, f32[16,512,1]{2,1,0:T(8,128)} %copy.39.scale_ref), custom_call_target="tpu_custom_call" | custom-call | tf_op jit(solution)/shard_map/pallas_call | solution.py:44
  215.3 11.5 %shard_map.83 = bf16[64,256,128]{2,1,0:T(8,128)(2,1)} custom-call(s32[64]{0:T(128)} %compare_select_fusion.source_ref, bf16[32,256,256]{2,1,0:T(8,128)(2,1)} %copy.40.left_ref, bf16[16,512,128]{2,1,0:T(8,128)(2,1)} %shard_map.82.flux_ref), custom_call_target="tpu_custom_call" | custom-call | tf_op jit(solution)/shard_map/pallas_call | solution.py:87
  226.8 19.1 %all-to-all-done.4 = bf16[32,512,128]{2,1,0:T(8,128)(2,1)} async-done(((bf16[32,512,128]{2,1,0:T(8,128)(2,1)}), bf16[32,512,128]{2,1,0:T(8,128)(2,1)}, u32[]{:S(2)}, u32[]{:S(2)}) %all-to-all-start.4) | async-done | bytes 4194336 | tf_op jit(solution)/shard_map/all_to_all | solution.py:249
  245.9 6.0 %all-to-all-start.2 = ((bf16[32,512,128]{2,1,0:T(8,128)(2,1)}), bf16[32,512,128]{2,1,0:T(8,128)(2,1)}, u32[]{:S(2)}, u32[]{:S(2)}) async-start(bf16[32,512,128]{2,1,0:T(8,128)(2,1)} %bitcast.98), calls=%async_computation.2 | async-start | bytes 8388608 | tf_op jit(solution)/shard_map/all_to_all | solution.py:249
  252.6 6.6 %shard_map.86.refs_0_ = f32[16,256,256]{2,1,0:T(8,128)} custom-call(s32[64]{0:T(128)} %sub.24.rows_ref, bf16[64,256,128]{2,1,0:T(8,128)(2,1)} %bitcast.32.tiles_ref), custom_call_target="tpu_custom_call" | custom-call | tf_op jit(solution)/shard_map/pallas_call | solution.py:130
  259.2 45.9 %all-to-all-done.2 = bf16[32,512,128]{2,1,0:T(8,128)(2,1)} async-done(((bf16[32,512,128]{2,1,0:T(8,128)(2,1)}), bf16[32,512,128]{2,1,0:T(8,128)(2,1)}, u32[]{:S(2)}, u32[]{:S(2)}) %all-to-all-start.2) | async-done | bytes 4194336 | tf_op jit(solution)/shard_map/all_to_all | solution.py:249
  305.1 6.6 %shard_map.87 = f32[16,256,256]{2,1,0:T(8,128)} custom-call(s32[64]{0:T(128)} %sub.24.rows_ref, bf16[64,256,128]{2,1,0:T(8,128)(2,1)} %bitcast.28.tiles_ref, f32[16,256,256]{2,1,0:T(8,128)} %shard_map.86.refs_0_), custom_call_target="tpu_custom_call", output_to_operand_aliasing={{}: (2, {})} | custom-call | tf_op jit(solution)/shard_map/pallas_call | solution.py:130
  (57 shorter events, 15.7 us)
Async XLA Ops:
  2.3 8.0 %copy-start.4 = (s32[32,1]{0,1:T(1,128)S(1)}, s32[32,1]{0,1:T(1,128)}, u32[]{:S(2)}) copy-start(s32[32,1]{0,1:T(1,128)} %param.14) | copy-start | bytes 388
  2.3 8.3 %copy-start.5 = (s32[32]{0:T(128)S(1)}, s32[32]{0:T(128)}, u32[]{:S(2)}) copy-start(s32[32]{0:T(128)} %param.15) | copy-start | bytes 388
  2.3 8.6 %collective-permute-start = (f32[512,69]{0,1:T(8,128)S(1)}, f32[512,69]{0,1:T(8,128)S(1)}, u32[]{:S(2)}, u32[]{:S(2)}) collective-permute-start(f32[512,69]{0,1:T(8,128)S(1)} %pad_maximum_fusion), channel_id=1, source_target_pairs={{96,0},{0,32},{32,64},{64,96},{97,1},{1,33},{33,65},{65,97},{98,2}... | collective-permute-start | bytes 423944 | tf_op jit(solution)/shard_map/ppermute | solution.py:20
  8.7 48.6 %collective-permute-start.1 = (bf16[512,16,128]{2,1,0:T(8,128)(2,1)}, bf16[512,16,128]{2,1,0:T(8,128)(2,1)}, u32[]{:S(2)}, u32[]{:S(2)}) collective-permute-start(bf16[512,16,128]{2,1,0:T(8,128)(2,1)} %get-tuple-element.29), channel_id=1, source_target_pairs={{96,0},{0,32},{32,64},{64,96},{97,1},{1,33},{33,65},{65,97},{98,2}... | collective-permute-start | bytes 6291464 | tf_op jit(solution)/shard_map/ppermute | solution.py:20
  14.9 18.4 %all-to-all-start = ((f32[32,1,2178]{2,1,0:T(1,128)}), f32[32,1,2178]{2,1,0:T(1,128)S(1)}, u32[]{:S(2)}, u32[]{:S(2)}) async-start(f32[32,1,2178]{2,1,0:T(1,128)} %copy.35), calls=%async_computation | async-start | bytes 589824 | tf_op jit(solution)/shard_map/all_to_all | solution.py:198
  23.1 5.9 %copy-start = (bf16[512,16,256]{2,1,0:T(8,128)(2,1)S(1)}, bf16[512,16,256]{2,1,0:T(8,128)(2,1)}, u32[]{:S(2)}) copy-start(bf16[512,16,256]{2,1,0:T(8,128)(2,1)} %param.12) | copy-start | bytes 12582916
  33.3 30.1 %copy-start.1 = (bf16[1024,512]{1,0:T(8,128)(2,1)}, bf16[1024,512]{1,0:T(8,128)(2,1)S(1)}, u32[]{:S(2)}) copy-start(bf16[1024,512]{1,0:T(8,128)(2,1)S(1)} %fusion.6) | copy-start | bytes 3145732
  63.3 62.8 %all-to-all-start.3 = ((bf16[32,32,2048]{2,1,0:T(8,128)(2,1)}), bf16[32,32,2048]{2,1,0:T(8,128)(2,1)}, u32[]{:S(2)}, u32[]{:S(2)}) async-start(bf16[32,32,2048]{2,1,0:T(8,128)(2,1)} %bitcast.100), calls=%async_computation.3 | async-start | bytes 8388608 | tf_op jit(solution)/shard_map/all_to_all | solution.py:241
  72.4 49.4 %collective-permute-start.2 = (bf16[512,16,128]{2,1,0:T(8,128)(2,1)}, bf16[512,16,128]{2,1,0:T(8,128)(2,1)S(1)}, u32[]{:S(2)}, u32[]{:S(2)}) collective-permute-start(bf16[512,16,128]{2,1,0:T(8,128)(2,1)} %get-tuple-element.15), channel_id=1, source_target_pairs={{96,0},{0,32},{32,64},{64,96},{97,1},{1,33},{33,65},{65,97},{98,2}... | collective-permute-start | bytes 6291464 | tf_op jit(solution)/shard_map/ppermute | solution.py:20
  73.0 24.2 %copy-start.3 = (f32[512]{0:T(512)S(1)}, f32[512]{0:T(512)}, u32[]{:S(2)}) copy-start(f32[512]{0:T(512)} %param.13) | copy-start | bytes 6148
  73.0 48.8 %copy-start.2 = (bf16[1024,512]{1,0:T(8,128)(2,1)S(1)}, bf16[1024,512]{1,0:T(8,128)(2,1)}, u32[]{:S(2)}) copy-start(bf16[1024,512]{1,0:T(8,128)(2,1)} %copy-done.1) | copy-start | bytes 3145732
  126.1 60.6 %all-to-all-start.1 = ((bf16[32,32,2048]{2,1,0:T(8,128)(2,1)}), bf16[32,32,2048]{2,1,0:T(8,128)(2,1)}, u32[]{:S(2)}, u32[]{:S(2)}) async-start(bf16[32,32,2048]{2,1,0:T(8,128)(2,1)} %bitcast.101), calls=%async_computation.1 | async-start | bytes 8388608 | tf_op jit(solution)/shard_map/all_to_all | solution.py:241
  186.7 59.2 %all-to-all-start.4 = ((bf16[32,512,128]{2,1,0:T(8,128)(2,1)}), bf16[32,512,128]{2,1,0:T(8,128)(2,1)}, u32[]{:S(2)}, u32[]{:S(2)}) async-start(bf16[32,512,128]{2,1,0:T(8,128)(2,1)} %bitcast.97), calls=%async_computation.4 | async-start | bytes 8388608 | tf_op jit(solution)/shard_map/all_to_all | solution.py:249
  245.9 59.2 %all-to-all-start.2 = ((bf16[32,512,128]{2,1,0:T(8,128)(2,1)}), bf16[32,512,128]{2,1,0:T(8,128)(2,1)}, u32[]{:S(2)}, u32[]{:S(2)}) async-start(bf16[32,512,128]{2,1,0:T(8,128)(2,1)} %bitcast.98), calls=%async_computation.2 | async-start | bytes 8388608 | tf_op jit(solution)/shard_map/all_to_all | solution.py:249

commit v7 on v2

--- a/solution.py
+++ b/solution.py
@@ -166,12 +166,14 @@
         ],
         axis=1,
     )
-    moved_meta = shifted(meta, "body", 1)
     moved_chunks = []
     for k in range(SPLIT):
         piece = master_basis[:, :, k * width:(k + 1) * width]
         if moved_chunks:
             piece, _ = lax.optimization_barrier((piece, moved_chunks[-1]))
+        else:
+            piece, meta = lax.optimization_barrier((piece, meta))
+            moved_meta = shifted(meta, "body", 1)
         moved_chunks.append(shifted(piece, "body", 1))
 
     moved_dest = moved_meta[:, wcols].astype(i32)

time: 311 us -> 312 us (level)
  transfers between devices with their start and end apart: 8 -> 8, of which waited for: 5 -> 6; matrix products, arithmetic and copies ran while one was open for 20% -> 19% of each run, Pallas kernels for 24% -> 23%
where the time goes in v7:
time: 312 us; the launch traced here: 311 us
  waiting for transfers between devices  123 us (39%)
  Pallas kernels  77.7 us (25%)
  starting transfers between devices  39.6 us (13%)
  other arithmetic  29.8 us (10%)
  local copies, waits for them, and re-layouts  28.2 us (9%)
  matrix products  12.1 us (4%)
    all_to_all x2, waiting for transfers between devices, on_device(): lax.all_to_all(packed_tiles.reshape(dom_count, tile_capacity * NP, width)...  66.8 us
    ppermute x3, waiting for transfers between devices, shifted(): return lax.ppermute(block, axis, route)  46.8 us
    pallas_call x2, Pallas kernels, flux_chunk(): pl.pallas_call(flux_kernel, grid=(q_count,), in_specs=[pl.BlockSpec((1, s...  45.1 us
    reduce_sum x1, other arithmetic, on_device(): weight_sum = jnp.sum(table, axis=2)  24.4 us
    pallas_call x2, Pallas kernels, packed_tiles_of(): pl.pallas_call(functools.partial(tile_kernel, tile_count, per_tile), in_s...  23.1 us
    all_to_all x2, starting transfers between devices, on_device(): lax.all_to_all(packed.reshape(dom_count, capacity, Q * width), 'dom', 0,...  15.7 us
    all_to_all x2, starting transfers between devices, on_device(): lax.all_to_all(packed_tiles.reshape(dom_count, tile_capacity * NP, width)...  12.1 us
    dot_general x2, matrix products, on_device(): jnp.dot(placer.astype(bf16), moved.reshape(seg_count, Q * width), preferr...  10.3 us
  transfers between devices with their start and end apart: 8, of which 6 were waited for; matrix products, arithmetic and copies ran while one was open for 19% of the time, Pallas kernels for 23%

profile of v7, /device:TPU:32, one launch (start us, length us, event | category | flops | bytes accessed | tf_op | source)
XLA Modules:
  0.0 310.6 jit_solution(10241216942694216618)
XLA Ops:
  2.3 4.3 %fusion.30 = (bf16[512,16,128]{2,1,0:T(8,128)(2,1)S(1)}, bf16[512,16,128]{2,1,0:T(8,128)(2,1)}) fusion(bf16[512,16,256]{2,1,0:T(8,128)(2,1)} %param.8), kind=kLoop, calls=%fused_computation.72 | loop fusion | bytes 8388608 | tf_op jit(solution)/shard_map/slice | solution.py:171
  10.2 4.3 %collective-permute-done = f32[512,69]{0,1:T(8,128)S(1)} collective-permute-done((f32[512,69]{0,1:T(8,128)S(1)}, f32[512,69]{0,1:T(8,128)S(1)}, u32[]{:S(2)}, u32[]{:S(2)}) %collective-permute-start) | collective-permute-done | bytes 141344 | tf_op jit(solution)/shard_map/ppermute | solution.py:20
  18.6 8.2 %all-to-all-start = ((f32[32,1,2178]{2,1,0:T(1,128)}), f32[32,1,2178]{2,1,0:T(1,128)S(1)}, u32[]{:S(2)}, u32[]{:S(2)}) async-start(f32[32,1,2178]{2,1,0:T(1,128)} %copy.35), calls=%async_computation | async-start | bytes 589824 | tf_op jit(solution)/shard_map/all_to_all | solution.py:197
  26.8 5.9 %copy.59 = bf16[512,16,256]{2,0,1:T(8,128)(2,1)} copy(bf16[512,16,256]{2,1,0:T(8,128)(2,1)} %param.12) | data formatting | bytes 8388608 | tf_op args[4]
  32.7 3.9 %copy.38 = bf16[32,256,16,16]{1,3,2,0:T(8,128)(2,1)} copy(bf16[32,256,16,16]{1,2,3,0:T(8,128)(2,1)S(1)} %bitcast.93) | data formatting | bytes 8388608 | tf_op jit(solution)/shard_map/transpose | solution.py:222
  40.2 18.3 %collective-permute-done.1 = bf16[512,16,128]{2,1,0:T(8,128)(2,1)} collective-permute-done((bf16[512,16,128]{2,1,0:T(8,128)(2,1)}, bf16[512,16,128]{2,1,0:T(8,128)(2,1)}, u32[]{:S(2)}, u32[]{:S(2)}) %collective-permute-start.1) | collective-permute-done | bytes 2097184 | tf_op jit(solution)/shard_map/ppermute | solution.py:20
  58.5 6.0 %convolution_convert_fusion = bf16[1024,2048]{1,0:T(8,128)(2,1)} fusion(bf16[64,8,16,128]{3,2,1,0:T(8,128)(2,1)} %bitcast.44, s32[512]{0:T(512)S(1)} %add.49), kind=kOutput, calls=%fused_computation.5 | convolution fusion | flops 2150105088 | bytes 6293504 | tf_op jit(solution)/shard_map/dot_general | solution.py:234
  64.5 8.3 %all-to-all-start.3 = ((bf16[32,32,2048]{2,1,0:T(8,128)(2,1)}), bf16[32,32,2048]{2,1,0:T(8,128)(2,1)}, u32[]{:S(2)}, u32[]{:S(2)}) async-start(bf16[32,32,2048]{2,1,0:T(8,128)(2,1)} %bitcast.98), calls=%async_computation.3 | async-start | bytes 8388608 | tf_op jit(solution)/shard_map/all_to_all | solution.py:240
  73.9 24.4 %fusion = (f32[16,512]{1,0:T(8,128)S(1)}, bf16[16,512,1024]{2,1,0:T(8,128)(2,1)}, bf16[16,512,1024]{2,1,0:T(8,128)(2,1)}) fusion(f32[16,1024]{1,0:T(8,128)} %get-tuple-element.39, f32[16,1024]{1,0:T(8,128)} %get-tuple-element.40, f32[16,1024]{1,0:T(8,128)} %get-tuple-element.41, f32[16,1024]{1,0:T(8,128)S(1)} %get-tuple-element.38, ...), kind=kLoop, calls=%fused_computation.2 | loop fusion | flops 100655104 | bytes 35946496 | tf_op jit(solution)/shard_map/reduce_sum | solution.py:213
  98.4 24.1 %collective-permute-done.2 = bf16[512,16,128]{2,1,0:T(8,128)(2,1)S(1)} collective-permute-done((bf16[512,16,128]{2,1,0:T(8,128)(2,1)S(1)}, bf16[512,16,128]{2,1,0:T(8,128)(2,1)S(1)}, u32[]{:S(2)}, u32[]{:S(2)}) %collective-permute-start.2) | collective-permute-done | bytes 2097184 | tf_op jit(solution)/shard_map/ppermute | solution.py:20
  122.5 4.3 %convolution_convert_fusion.1 = bf16[1024,2048]{1,0:T(8,128)(2,1)} fusion(bf16[64,8,16,128]{3,2,1,0:T(8,128)(2,1)S(1)} %bitcast.108, s32[512]{0:T(512)S(1)} %add.49), kind=kOutput, calls=%fused_computation.6 | convolution fusion | flops 2150105088 | bytes 6293504 | tf_op jit(solution)/shard_map/dot_general | solution.py:234
  126.8 7.4 %all-to-all-start.1 = ((bf16[32,32,2048]{2,1,0:T(8,128)(2,1)}), bf16[32,32,2048]{2,1,0:T(8,128)(2,1)}, u32[]{:S(2)}, u32[]{:S(2)}) async-start(bf16[32,32,2048]{2,1,0:T(8,128)(2,1)} %bitcast.99), calls=%async_computation.1 | async-start | bytes 8388608 | tf_op jit(solution)/shard_map/all_to_all | solution.py:240
  135.0 6.4 %copy.40.left_ref = bf16[32,256,256]{2,1,0:T(8,128)(2,1)} copy(bf16[32,256,256]{1,2,0:T(8,128)(2,1)} %bitcast.94) | data formatting | bytes 8388608 | tf_op jit(solution)/shard_map/optimization_barrier | solution.py:231
  144.1 22.5 %shard_map.84.flux_ref = bf16[16,512,128]{2,1,0:T(8,128)(2,1)} custom-call(bf16[16,512,1024]{2,1,0:T(8,128)(2,1)} %get-tuple-element.24.hi_ref, bf16[16,512,1024]{2,1,0:T(8,128)(2,1)} %get-tuple-element.25.lo_ref, bf16[1024,2048]{1,0:T(8,128)(2,1)} %bitcast.30.rows_ref, bf16[16,512,256]{2,1,0:T(8,128)(2,1)} %bitcast.91, f32[16,512,1]{2,1,0:T(8,128)} %copy.39.scale_ref), custom_call_target="tpu_custom_call" | custom-call | tf_op jit(solution)/shard_map/pallas_call | solution.py:44
  166.6 11.6 %shard_map.85 = bf16[64,256,128]{2,1,0:T(8,128)(2,1)} custom-call(s32[64]{0:T(128)} %compare_select_fusion.source_ref, bf16[32,256,256]{2,1,0:T(8,128)(2,1)} %copy.40.left_ref, bf16[16,512,128]{2,1,0:T(8,128)(2,1)} %shard_map.84.flux_ref), custom_call_target="tpu_custom_call" | custom-call | tf_op jit(solution)/shard_map/pallas_call | solution.py:87
  178.2 9.2 %all-to-all-done.1 = bf16[32,32,2048]{2,1,0:T(8,128)(2,1)} async-done(((bf16[32,32,2048]{2,1,0:T(8,128)(2,1)}), bf16[32,32,2048]{2,1,0:T(8,128)(2,1)}, u32[]{:S(2)}, u32[]{:S(2)}) %all-to-all-start.1) | async-done | bytes 4194336 | tf_op jit(solution)/shard_map/all_to_all | solution.py:240
  187.4 6.0 %all-to-all-start.4 = ((bf16[32,512,128]{2,1,0:T(8,128)(2,1)}), bf16[32,512,128]{2,1,0:T(8,128)(2,1)}, u32[]{:S(2)}, u32[]{:S(2)}) async-start(bf16[32,512,128]{2,1,0:T(8,128)(2,1)} %bitcast.95), calls=%async_computation.4 | async-start | bytes 8388608 | tf_op jit(solution)/shard_map/all_to_all | solution.py:248
  193.5 22.6 %shard_map.82.flux_ref = bf16[16,512,128]{2,1,0:T(8,128)(2,1)} custom-call(bf16[16,512,1024]{2,1,0:T(8,128)(2,1)} %get-tuple-element.24.hi_ref, bf16[16,512,1024]{2,1,0:T(8,128)(2,1)} %get-tuple-element.25.lo_ref, bf16[1024,2048]{1,0:T(8,128)(2,1)} %bitcast.26.rows_ref, bf16[16,512,256]{2,1,0:T(8,128)(2,1)} %bitcast.92, f32[16,512,1]{2,1,0:T(8,128)} %copy.39.scale_ref), custom_call_target="tpu_custom_call" | custom-call | tf_op jit(solution)/shard_map/pallas_call | solution.py:44
  216.1 11.5 %shard_map.83 = bf16[64,256,128]{2,1,0:T(8,128)(2,1)} custom-call(s32[64]{0:T(128)} %compare_select_fusion.source_ref, bf16[32,256,256]{2,1,0:T(8,128)(2,1)} %copy.40.left_ref, bf16[16,512,128]{2,1,0:T(8,128)(2,1)} %shard_map.82.flux_ref), custom_call_target="tpu_custom_call" | custom-call | tf_op jit(solution)/shard_map/pallas_call | solution.py:87
  227.5 19.1 %all-to-all-done.4 = bf16[32,512,128]{2,1,0:T(8,128)(2,1)} async-done(((bf16[32,512,128]{2,1,0:T(8,128)(2,1)}), bf16[32,512,128]{2,1,0:T(8,128)(2,1)}, u32[]{:S(2)}, u32[]{:S(2)}) %all-to-all-start.4) | async-done | bytes 4194336 | tf_op jit(solution)/shard_map/all_to_all | solution.py:248
  246.6 6.0 %all-to-all-start.2 = ((bf16[32,512,128]{2,1,0:T(8,128)(2,1)}), bf16[32,512,128]{2,1,0:T(8,128)(2,1)}, u32[]{:S(2)}, u32[]{:S(2)}) async-start(bf16[32,512,128]{2,1,0:T(8,128)(2,1)} %bitcast.96), calls=%async_computation.2 | async-start | bytes 8388608 | tf_op jit(solution)/shard_map/all_to_all | solution.py:248
  253.3 4.8 %shard_map.86.refs_0_ = f32[16,256,256]{2,1,0:T(8,128)} custom-call(s32[64]{0:T(128)} %sub.24.rows_ref, bf16[64,256,128]{2,1,0:T(8,128)(2,1)} %bitcast.32.tiles_ref), custom_call_target="tpu_custom_call" | custom-call | tf_op jit(solution)/shard_map/pallas_call | solution.py:128
  258.1 47.7 %all-to-all-done.2 = bf16[32,512,128]{2,1,0:T(8,128)(2,1)} async-done(((bf16[32,512,128]{2,1,0:T(8,128)(2,1)}), bf16[32,512,128]{2,1,0:T(8,128)(2,1)}, u32[]{:S(2)}, u32[]{:S(2)}) %all-to-all-start.2) | async-done | bytes 4194336 | tf_op jit(solution)/shard_map/all_to_all | solution.py:248
  305.9 4.8 %shard_map.87 = f32[16,256,256]{2,1,0:T(8,128)} custom-call(s32[64]{0:T(128)} %sub.24.rows_ref, bf16[64,256,128]{2,1,0:T(8,128)(2,1)} %bitcast.28.tiles_ref, f32[16,256,256]{2,1,0:T(8,128)} %shard_map.86.refs_0_), custom_call_target="tpu_custom_call", output_to_operand_aliasing={{}: (2, {})} | custom-call | tf_op jit(solution)/shard_map/pallas_call | solution.py:128
  (52 shorter events, 18.6 us)
Async XLA Ops:
  2.2 7.4 %copy-start.2 = (s32[32,1]{0,1:T(1,128)S(1)}, s32[32,1]{0,1:T(1,128)}, u32[]{:S(2)}) copy-start(s32[32,1]{0,1:T(1,128)} %param.14) | copy-start | bytes 388
  2.2 7.7 %copy-start.3 = (s32[32]{0:T(128)S(1)}, s32[32]{0:T(128)}, u32[]{:S(2)}) copy-start(s32[32]{0:T(128)} %param.15) | copy-start | bytes 388
  6.6 8.0 %collective-permute-start = (f32[512,69]{0,1:T(8,128)S(1)}, f32[512,69]{0,1:T(8,128)S(1)}, u32[]{:S(2)}, u32[]{:S(2)}) collective-permute-start(f32[512,69]{0,1:T(8,128)S(1)} %pad_maximum_fusion), channel_id=1, source_target_pairs={{96,0},{0,32},{32,64},{64,96},{97,1},{1,33},{33,65},{65,97},{98,2}... | collective-permute-start | bytes 423944 | tf_op jit(solution)/shard_map/ppermute | solution.py:20
  8.1 50.4 %collective-permute-start.1 = (bf16[512,16,128]{2,1,0:T(8,128)(2,1)}, bf16[512,16,128]{2,1,0:T(8,128)(2,1)}, u32[]{:S(2)}, u32[]{:S(2)}) collective-permute-start(bf16[512,16,128]{2,1,0:T(8,128)(2,1)} %get-tuple-element.18), channel_id=1, source_target_pairs={{96,0},{0,32},{32,64},{64,96},{97,1},{1,33},{33,65},{65,97},{98,2}... | collective-permute-start | bytes 6291464 | tf_op jit(solution)/shard_map/ppermute | solution.py:20
  18.6 18.0 %all-to-all-start = ((f32[32,1,2178]{2,1,0:T(1,128)}), f32[32,1,2178]{2,1,0:T(1,128)S(1)}, u32[]{:S(2)}, u32[]{:S(2)}) async-start(f32[32,1,2178]{2,1,0:T(1,128)} %copy.35), calls=%async_computation | async-start | bytes 589824 | tf_op jit(solution)/shard_map/all_to_all | solution.py:197
  26.8 5.9 %copy-start = (bf16[512,16,256]{2,1,0:T(8,128)(2,1)S(1)}, bf16[512,16,256]{2,1,0:T(8,128)(2,1)}, u32[]{:S(2)}) copy-start(bf16[512,16,256]{2,1,0:T(8,128)(2,1)} %param.12) | copy-start | bytes 12582916
  64.5 62.4 %all-to-all-start.3 = ((bf16[32,32,2048]{2,1,0:T(8,128)(2,1)}), bf16[32,32,2048]{2,1,0:T(8,128)(2,1)}, u32[]{:S(2)}, u32[]{:S(2)}) async-start(bf16[32,32,2048]{2,1,0:T(8,128)(2,1)} %bitcast.98), calls=%async_computation.3 | async-start | bytes 8388608 | tf_op jit(solution)/shard_map/all_to_all | solution.py:240
  73.4 49.2 %collective-permute-start.2 = (bf16[512,16,128]{2,1,0:T(8,128)(2,1)S(1)}, bf16[512,16,128]{2,1,0:T(8,128)(2,1)S(1)}, u32[]{:S(2)}, u32[]{:S(2)}) collective-permute-start(bf16[512,16,128]{2,1,0:T(8,128)(2,1)S(1)} %get-tuple-element.19), channel_id=1, source_target_pairs={{96,0},{0,32},{32,64},{64,96},{97,1},{1,33},{33,65},{65,97},{98,2}... | collective-permute-start | bytes 6291464 | tf_op jit(solution)/shard_map/ppermute | solution.py:20
  73.9 24.4 %copy-start.1 = (f32[512]{0:T(512)S(1)}, f32[512]{0:T(512)}, u32[]{:S(2)}) copy-start(f32[512]{0:T(512)} %param.13) | copy-start | bytes 6148
  126.8 60.6 %all-to-all-start.1 = ((bf16[32,32,2048]{2,1,0:T(8,128)(2,1)}), bf16[32,32,2048]{2,1,0:T(8,128)(2,1)}, u32[]{:S(2)}, u32[]{:S(2)}) async-start(bf16[32,32,2048]{2,1,0:T(8,128)(2,1)} %bitcast.99), calls=%async_computation.1 | async-start | bytes 8388608 | tf_op jit(solution)/shard_map/all_to_all | solution.py:240
  187.4 59.2 %all-to-all-start.4 = ((bf16[32,512,128]{2,1,0:T(8,128)(2,1)}), bf16[32,512,128]{2,1,0:T(8,128)(2,1)}, u32[]{:S(2)}, u32[]{:S(2)}) async-start(bf16[32,512,128]{2,1,0:T(8,128)(2,1)} %bitcast.95), calls=%async_computation.4 | async-start | bytes 8388608 | tf_op jit(solution)/shard_map/all_to_all | solution.py:248
  246.6 59.2 %all-to-all-start.2 = ((bf16[32,512,128]{2,1,0:T(8,128)(2,1)}), bf16[32,512,128]{2,1,0:T(8,128)(2,1)}, u32[]{:S(2)}, u32[]{:S(2)}) async-start(bf16[32,512,128]{2,1,0:T(8,128)(2,1)} %bitcast.96), calls=%async_computation.2 | async-start | bytes 8388608 | tf_op jit(solution)/shard_map/all_to_all | solution.py:248
